TPU v7x, 512 devices: a whole 4x4x16 slice. The times are simulated.
512 devices in a mesh: inst: 16 (over y_lo, x, core), blk: 32 (over z, y_hi).
Axes of the slice: x: 4, y: 4 (y_hi: 2, y_lo: 2; y = y_hi * 2 + y_lo), z: 16, core: 2. Of those that a mesh axis runs over, the one named last changes fastest.
Arguments:
- state: float32 [16, 2, 6, 8, 8, 4096], P('inst', None, None, None, None, 'blk'), may hold values from -0.5 to 3, as said below
- donor_block: int32 [16, 2, 32], P('inst', None, 'blk'), may hold values from 0 to 31, as said below
- donor_offset: int32 [16, 2, 32], P('inst', None, 'blk'), may hold values from 0 to 127, as said below
Outputs:
- hb_residual: float32 [16, 2, 6, 8, 8, 4096], P('inst', None, None, None, None, 'blk')
- new_state: float32 [16, 2, 6, 8, 8, 4096], P('inst', None, None, None, None, 'blk')
Inputs may be any that keep to these rules, and one draw needn't show every extreme that they name: For each instance n and row r there is one rotation R with donor_block[n, r, b] = (b + R) mod 32 for every block b. `donor_offset`: for each instance and row the offset is the same for all blocks. `state`: density lies in [0.8, 1.25], momenta in [-0.5, 0.5], total energy in [2, 3], turbulence variable in [0.05, 0.5].
All inputs are finite; a program needn't handle non-finite values.
Results may differ from a plain program's by a relative error of at most 0.0003.
Values sent between devices are 32-bit elements; how exact they have to be, the bound alone decides.
No kernel may reach another device: no remote copies, remote signals or barrier semaphores. Data moves between devices by JAX's collectives and lax.ppermute only.
A program may use at most 64 MiB of HBM per device.

v0:
```python
import jax
import jax.numpy as jnp
from jax import lax
from jax.sharding import PartitionSpec as P

gamma_ratio = 1.4
second_coef = 0.5
fourth_coef = 1.0 / 32.0
courant = 0.8
frequency = 0.5
highest = lax.Precision.HIGHEST


def spectral_weights(target, source, number):
    distance = jnp.mod(target - source, number)
    angle = jnp.pi / number * distance.astype(jnp.float32)
    parity = 1.0 - 2.0 * jnp.mod(distance, 2).astype(jnp.float32)
    nonzero = distance != 0
    sine_safe = jnp.where(nonzero, jnp.sin(angle), 1.0)
    cotangent = jnp.where(nonzero, jnp.cos(angle) / sine_safe, 0.0)
    return parity * (0.25 * frequency + 0.5 * frequency * cotangent)


def take_range(array, begin, length, along):
    return lax.slice_in_dim(array, begin, begin + length, axis=along)


def flux_divergence(extended, along):
    length = extended.shape[along] - 4
    cell_axis = along - 1
    density = extended[0]
    inverse = 1.0 / density
    normal_vel = extended[along] * inverse
    kinetic = 0.5 * (extended[1] ** 2 + extended[2] ** 2 + extended[3] ** 2) * inverse
    pressure = (gamma_ratio - 1.0) * (extended[4] - kinetic)
    sound = jnp.sqrt(gamma_ratio * pressure * inverse)
    momentum_flux = []
    for component in (1, 2, 3):
        if component == along:
            momentum_flux.append(extended[component] * normal_vel + pressure)
        else:
            momentum_flux.append(extended[component] * normal_vel)
    fluxes = jnp.stack(
        [extended[along]]
        + momentum_flux
        + [(extended[4] + pressure) * normal_vel, extended[5] * normal_vel]
    )
    radius = jnp.abs(normal_vel) + sound
    p_plus = take_range(pressure, 2, length + 2, cell_axis)
    p_here = take_range(pressure, 1, length + 2, cell_axis)
    p_minus = take_range(pressure, 0, length + 2, cell_axis)
    sensor = jnp.abs(p_plus - 2.0 * p_here + p_minus) / (p_plus + 2.0 * p_here + p_minus)
    spread = 0.5 * (
        take_range(radius, 1, length + 1, cell_axis) + take_range(radius, 2, length + 1, cell_axis)
    )
    eps_two = second_coef * jnp.maximum(
        take_range(sensor, 0, length + 1, cell_axis), take_range(sensor, 1, length + 1, cell_axis)
    )
    eps_four = jnp.maximum(0.0, fourth_coef - eps_two)
    first_diff = take_range(extended, 2, length + 1, along) - take_range(
        extended, 1, length + 1, along
    )
    third_diff = (
        take_range(extended, 3, length + 1, along)
        - 3.0 * take_range(extended, 2, length + 1, along)
        + 3.0 * take_range(extended, 1, length + 1, along)
        - take_range(extended, 0, length + 1, along)
    )
    interface = 0.5 * (
        take_range(fluxes, 1, length + 1, along) + take_range(fluxes, 2, length + 1, along)
    ) - spread * (eps_two * first_diff - eps_four * third_diff)
    return take_range(interface, 1, length, along) - take_range(interface, 0, length, along)


def wall_extend(block):
    mirror_sign = jnp.array([1.0, 1.0, -1.0, 1.0, 1.0, 1.0], jnp.float32).reshape(6, 1, 1, 1)
    lower_ghost = block[:, :, 0:2][:, :, ::-1] * mirror_sign
    upper_ghost = block[:, :, -2:][:, :, ::-1] * mirror_sign
    return jnp.concatenate([lower_ghost, block, upper_ghost], axis=2)


def row_residual(block, low_ghost, high_ghost, circum_ext):
    axial_ext = jnp.concatenate([low_ghost, block, high_ghost], axis=1)
    return (
        flux_divergence(axial_ext, 1)
        + flux_divergence(wall_extend(block), 2)
        + flux_divergence(circum_ext, 3)
    )


def local_step(fields, number):
    inverse = 1.0 / fields[:, 0]
    kinetic = 0.5 * (fields[:, 1] ** 2 + fields[:, 2] ** 2 + fields[:, 3] ** 2) * inverse
    pressure = (gamma_ratio - 1.0) * (fields[:, 4] - kinetic)
    sound = jnp.sqrt(gamma_ratio * pressure * inverse)
    speeds = (jnp.abs(fields[:, 1]) + jnp.abs(fields[:, 2]) + jnp.abs(fields[:, 3])) * inverse
    return courant / (speeds + 3.0 * sound + frequency * number / 2.0)


def shifted(payloads, shift):
    count = lax.axis_size("blk")
    pairs = [(source, (source - shift) % count) for source in range(count)]
    rows = [p.reshape(-1, 128) for p in payloads]
    sizes = [r.shape[0] for r in rows]
    moved = lax.ppermute(jnp.concatenate(rows, axis=0) if len(rows) > 1 else rows[0], "blk", pairs)
    pieces, begin = [], 0
    for p, size in zip(payloads, sizes):
        pieces.append(moved[begin:begin + size].reshape(p.shape))
        begin += size
    return pieces


def pick(candidates, index):
    chosen = candidates[0]
    for k in range(1, len(candidates)):
        chosen = jnp.where(index == k, candidates[k], chosen)
    return chosen


def cut_window(first, second, offset):
    width = first.shape[-1]
    joined = jnp.concatenate([first, second], axis=-1).reshape(-1, 2 * width)
    rows = lax.broadcasted_iota(jnp.int32, (2 * width, width), 0)
    cols = lax.broadcasted_iota(jnp.int32, (2 * width, width), 1)
    selection = (rows == cols + offset).astype(jnp.float32)
    return jnp.dot(joined, selection, precision=highest).reshape(first.shape)


def signed_digit(value, radix):
    return jnp.mod(value + 1, radix) - 1


def per_device(state, donor_block, donor_offset):
    number = lax.axis_size("inst")
    total_blocks = lax.axis_size("blk")
    own_instance = lax.axis_index("inst")
    own_block = lax.axis_index("blk")
    fields = state[0]
    faces = jnp.stack([fields[1, :, 0:2], fields[0, :, -2:]])
    faces_below, halo_low = shifted([faces, fields[..., -2:]], -1)
    faces_above, halo_high = shifted([faces, fields[..., :2]], 1)
    near = [faces_below, faces, faces_above] + [shifted([faces], s)[0] for s in (2, 3)]
    padded = jnp.concatenate([halo_low, fields, halo_high], axis=-1)
    windows, far_digit, top_digit = [], [], []
    for t in range(2):
        rotation = jnp.mod(donor_block[0, t, 0] - own_block, total_blocks)
        low = signed_digit(rotation, 4)
        rest = jnp.mod((rotation - low) // 4, total_blocks // 4)
        far_digit.append(signed_digit(rest, 4))
        top_digit.append(jnp.mod((rest - far_digit[t]) // 4, 2))
        first = pick([c[t] for c in near], low + 1)
        second = pick([c[t] for c in near], low + 2)
        windows.append(cut_window(first, second, donor_offset[0, t, 0]))
    windows = jnp.stack(windows)
    far = [shifted([windows], -4)[0], windows] + [shifted([windows], s)[0] for s in (4, 8)]
    windows = jnp.stack([pick([c[t] for c in far], far_digit[t] + 1) for t in range(2)])
    top = shifted([windows], 16)[0]
    rotor_high, stator_low = [jnp.where(top_digit[t] == 1, top[t], windows[t]) for t in range(2)]
    piece = lax.all_gather(state, "inst", axis=0, tiled=True)
    sources = jnp.arange(piece.shape[0], dtype=jnp.int32)
    weights = spectral_weights(own_instance, sources, number)
    spectral = jnp.sum(weights.reshape((-1,) + (1,) * (piece.ndim - 1)) * piece, axis=0)
    rotor = fields[0]
    stator = fields[1]
    rotor_low = jnp.concatenate([rotor[:, 0:1], rotor[:, 0:1]], axis=1)
    stator_high = jnp.concatenate([stator[:, -1:], stator[:, -1:]], axis=1)
    rotor_res = row_residual(rotor, rotor_low, rotor_high, padded[0])
    stator_res = row_residual(stator, stator_low, stator_high, padded[1])
    step = local_step(fields, number)
    residual = jnp.stack([rotor_res, stator_res]) + spectral
    updated = fields - step[:, None] * residual
    return (residual[None], updated[None])


def solution(mesh):
    return jax.shard_map(
        per_device,
        mesh=mesh,
        in_specs=(
            P("inst", None, None, None, None, "blk"),
            P("inst", None, "blk"),
            P("inst", None, "blk"),
        ),
        out_specs=(
            P("inst", None, None, None, None, "blk"),
            P("inst", None, None, None, None, "blk"),
        ),
        check_vma=False,
    )
```

profile of v0, /device:TPU:4, one launch (start us, length us, event | category | flops | bytes accessed | tf_op | source)
XLA Modules:
  0.0 102.8 jit_solution(11553175732543524007)
XLA Ops:
  7.2 0.7 all-gather.2.cloned.1.call-update
  7.9 0.8 fusion.159
  8.8 0.1 copy.19
  8.9 11.4 %collective-permute-start.1 = (f32[192,128]{0,1:T(8,128)S(1)}, f32[192,128]{0,1:T(8,128)}, u32[]{:S(2)}, u32[]{:S(2)}) collective-permute-start(f32[192,128]{0,1:T(8,128)S(1)} %copy.19), channel_id=1, source_target_pairs={{0,30},{1,31},{2,0},{3,1},{4,2},{5,3},{6,4},{7,5},{8,6},{9,7},{10,... | collective-permute-start | bytes 294920 | tf_op jit(solution)/shard_map/ppermute | solution.py:105
  20.3 6.0 %collective-permute-start = (f32[192,128]{0,1:T(8,128)S(1)}, f32[192,128]{0,1:T(8,128)}, u32[]{:S(2)}, u32[]{:S(2)}) collective-permute-start(f32[192,128]{0,1:T(8,128)S(1)} %copy.19), channel_id=1, source_target_pairs={{0,29},{1,30},{2,31},{3,0},{4,1},{5,2},{6,3},{7,4},{8,5},{9,6},{10... | collective-permute-start | bytes 294920 | tf_op jit(solution)/shard_map/ppermute | solution.py:105
  26.3 1.3 %fusion.158 = (f32[2,6,8,8,2]{4,3,2,1,0:T(8,128)S(1)}, f32[2,6,8,8,2]{4,3,2,1,0:T(8,128)S(1)}) fusion(f32[2,6,8,8,128]{4,3,2,1,0:T(8,128)} %bitcast.368), kind=kLoop, calls=%fused_computation.368 | loop fusion | bytes 24576 | tf_op jit(solution)/shard_map/slice | solution.py:140
  27.6 0.2 reshape.707
  27.8 0.2 reshape.706
  28.0 0.1 copy.31
  28.1 0.1 copy.32
  28.2 0.8 pad_maximum_fusion.17
  29.0 1.9 %collective-permute-start.3 = (f32[204,128]{0,1:T(8,128)}, f32[204,128]{0,1:T(8,128)S(1)}, u32[]{:S(2)}, u32[]{:S(2)}) collective-permute-start(f32[204,128]{0,1:T(8,128)} %get-tuple-element.77), channel_id=1, source_target_pairs={{0,1},{1,2},{2,3},{3,4},{4,5},{5,6},{6,7},{7,8},{8,9},{9,10},{10,1... | collective-permute-start | bytes 313352 | tf_op jit(solution)/shard_map/ppermute | solution.py:105
  31.0 7.5 %collective-permute-start.2 = (f32[204,128]{0,1:T(8,128)}, f32[204,128]{0,1:T(8,128)S(1)}, u32[]{:S(2)}, u32[]{:S(2)}) collective-permute-start(f32[204,128]{0,1:T(8,128)} %get-tuple-element.78), channel_id=1, source_target_pairs={{0,31},{1,0},{2,1},{3,2},{4,3},{5,4},{6,5},{7,6},{8,7},{9,8},{10,9... | collective-permute-start | bytes 313352 | tf_op jit(solution)/shard_map/ppermute | solution.py:105
  38.5 1.4 %fusion.166 = (s32[1,1,1]{1,2,0:T(1,128)}, s32[1,1,1]{1,2,0:T(1,128)}) fusion(s32[1,2,1]{1,2,0:T(1,128)} %param.6), kind=kLoop, calls=%fused_computation.376 | loop fusion | bytes 16 | tf_op jit(solution)/shard_map/slice | solution.py:146
  41.5 1.1 %fusion.118 = f32[2,8,8,128]{3,2,1,0:T(8,128)S(1)} fusion(f32[2,6,8,8,128]{4,3,2,1,0:T(8,128)} %bitcast.369), kind=kLoop, calls=%fused_computation.280 | loop fusion | flops 344064 | bytes 393216 | tf_op jit(solution)/shard_map/mul | solution.py:171
  42.5 1.1 %slice_bitcast_fusion.3 = (f32[6,8,8,128]{3,2,1,0:T(8,128)S(1)}, f32[6,8,8,128]{3,2,1,0:T(8,128)S(1)}) fusion(f32[1,2,6,8,8,128]{5,4,3,2,1,0:T(8,128)} %param.5), kind=kLoop, calls=%fused_computation.99 | loop fusion | bytes 786432 | tf_op jit(solution)/shard_map/squeeze | solution.py:163
  43.7 0.1 rev.13
  43.8 0.1 rev.12
  43.9 0.1 rev.15
  44.1 0.1 rev.14
  44.2 0.1 broadcast_multiply_fusion.6
  44.3 0.1 pad_maximum_fusion.5
  44.5 0.1 fusion.114
  44.6 0.6 fusion.139
  45.3 1.3 %fusion.165 = (s32[1,1,1]{1,2,0:T(1,128)}, s32[1,1,1]{1,2,0:T(1,128)}) fusion(s32[1,2,1]{1,2,0:T(1,128)} %param.7), kind=kLoop, calls=%fused_computation.375 | loop fusion | bytes 16 | tf_op jit(solution)/shard_map/slice | solution.py:153
  46.6 1.3 %iota_add_fusion.1 = s32[128]{0:T(128)} fusion(s32[]{:T(128)} %bitcast.5), kind=kLoop, calls=%fused_computation.365 | loop fusion | flops 128 | bytes 516 | tf_op jit(solution)/shard_map/add | solution.py:125
  47.8 0.1 copy.27
  48.0 0.1 copy.25
  48.5 0.4 fusion.24
  48.9 0.4 fusion.10
  49.3 0.6 iota_add_fusion
  49.9 0.9 select_select_fusion.3
  50.8 0.3 fusion.53
  51.1 1.1 %select_select_fusion.1 = (f32[96,128]{0,1:T(8,128)S(1)}, f32[96,128]{0,1:T(8,128)S(1)}) fusion(f32[96,128]{0,1:T(8,128)S(1)} %copy.27, f32[204,128]{0,1:T(8,128)S(1)} %collective-permute-done.3, f32[204,128]{0,1:T(8,128)S(1)} %collective-permute-done.2, f32[192,128]{0,1:T(8,128)} %collective-permute-done.1, f32[192,128]{0,1:T(8,128)} %collective-permute-done, ...), kind=kLoop, calls=%fused_computation.276 | loop fusion | flops 98304 | bytes 344072 | tf_op jit(solution)/shard_map/jit(_where)/select_n | solution.py:116
  52.2 0.3 fusion.57
  52.5 2.2 %collective-permute-start.6 = (f32[192,128]{1,0:T(8,128)S(1)}, f32[192,128]{1,0:T(8,128)S(1)}, u32[]{:S(2)}, u32[]{:S(2)}) collective-permute-start(f32[192,128]{1,0:T(8,128)S(1)} %bitcast.388), channel_id=1, source_target_pairs={{0,4},{1,5},{2,6},{3,7},{4,8},{5,9},{6,10},{7,11},{8,12},{9,13},{1... | collective-permute-start | bytes 294920 | tf_op jit(solution)/shard_map/ppermute | solution.py:105
  54.7 5.8 %collective-permute-start.5 = (f32[192,128]{1,0:T(8,128)S(1)}, f32[192,128]{1,0:T(8,128)S(1)}, u32[]{:S(2)}, u32[]{:S(2)}) collective-permute-start(f32[192,128]{1,0:T(8,128)S(1)} %bitcast.389), channel_id=1, source_target_pairs={{0,28},{1,29},{2,30},{3,31},{4,0},{5,1},{6,2},{7,3},{8,4},{9,5},{1... | collective-permute-start | bytes 294920 | tf_op jit(solution)/shard_map/ppermute | solution.py:105
  60.5 5.5 %collective-permute-start.4 = (f32[192,128]{1,0:T(8,128)S(1)}, f32[192,128]{1,0:T(8,128)S(1)}, u32[]{:S(2)}, u32[]{:S(2)}) collective-permute-start(f32[192,128]{1,0:T(8,128)S(1)} %bitcast.390), channel_id=1, source_target_pairs={{0,24},{1,25},{2,26},{3,27},{4,28},{5,29},{6,30},{7,31},{8,0},{9,1... | collective-permute-start | bytes 294920 | tf_op jit(solution)/shard_map/ppermute | solution.py:105
  65.9 0.1 slice.855
  66.0 0.1 reshape.704
  66.2 0.1 slice.856
  66.2 0.1 reshape.705
  66.4 1.1 %copy.30 = f32[2,6,8,8,2]{4,3,2,1,0:T(8,128)S(1)} copy(f32[2,6,8,8,2]{1,0,4,3,2:T(2,128)S(1)} %reshape.705) | data formatting | bytes 12288 | tf_op jit(solution)/shard_map/reshape | solution.py:108
  67.5 1.1 %copy.29 = f32[2,6,8,8,2]{4,3,2,1,0:T(8,128)S(1)} copy(f32[2,6,8,8,2]{1,0,4,3,2:T(2,128)S(1)} %reshape.704) | data formatting | bytes 12288 | tf_op jit(solution)/shard_map/reshape | solution.py:108
  68.6 0.4 pad_maximum_fusion
  69.0 0.1 fusion.101
  69.1 0.1 fusion.74
  69.3 0.1 add_divide_fusion.2
  69.4 0.1 add_divide_fusion
  69.5 0.1 subtract_maximum_fusion
  69.6 0.1 subtract_maximum_fusion.2
  69.9 0.1 slice_bitcast_fusion.1
  70.0 0.1 fusion.69
  70.1 0.4 collective-permute-done.5
  70.5 3.4 %collective-permute-done.4 = f32[192,128]{1,0:T(8,128)S(1)} collective-permute-done((f32[192,128]{1,0:T(8,128)S(1)}, f32[192,128]{1,0:T(8,128)S(1)}, u32[]{:S(2)}, u32[]{:S(2)}) %collective-permute-start.4) | collective-permute-done | bytes 98336 | tf_op jit(solution)/shard_map/ppermute | solution.py:105
  74.0 8.9 %collective-permute-start.7 = (f32[192,128]{1,0:T(8,128)S(1)}, f32[192,128]{1,0:T(8,128)S(1)}, u32[]{:S(2)}, u32[]{:S(2)}) collective-permute-start(f32[192,128]{1,0:T(8,128)S(1)} %bitcast.391), channel_id=1, source_target_pairs={{0,16},{1,17},{2,18},{3,19},{4,20},{5,21},{6,22},{7,23},{8,24},{9,... | collective-permute-start | bytes 294920 | tf_op jit(solution)/shard_map/ppermute | solution.py:105
  82.9 1.1 %fusion.3 = (f32[6,8,8,129]{3,2,1,0:T(8,128)S(1)}, f32[6,8,8,129]{3,2,1,0:T(8,128)S(1)}) fusion(f32[6,8,8,132]{3,2,1,0:T(8,128)S(1)} %get-tuple-element.60, f32[6,8,8,132]{3,2,1,0:T(8,128)S(1)} %constant_dynamic-update-slice_fusion.30, f32[8,8,129]{2,1,0:T(8,128)S(1)} %get-tuple-element.44, f32[8,8,129]{2,1,0:T(8,128)S(1)} %get-tuple-element.45, ...), kind=kLoop, calls=%fused_computation.6 | loop fusion | flops 1287936 | bytes 2972160 | tf_op jit(solution)/shard_map/sub | solution.py:69
  84.0 6.3 %collective-permute-done.7 = f32[192,128]{1,0:T(8,128)S(1)} collective-permute-done((f32[192,128]{1,0:T(8,128)S(1)}, f32[192,128]{1,0:T(8,128)S(1)}, u32[]{:S(2)}, u32[]{:S(2)}) %collective-permute-start.7) | collective-permute-done | bytes 98336 | tf_op jit(solution)/shard_map/ppermute | solution.py:105
  90.9 0.1 fusion.42
  91.0 0.1 fusion.36
  91.1 0.1 fusion.51
  91.2 0.1 fusion.48
  91.4 3.6 %multiply_reduce_fusion = f32[2,6,8,8,128]{4,3,2,1,0:T(8,128)S(1)} fusion(f32[16,2,6,8,8,128]{5,4,3,2,1,0:T(8,128)} %all-gather.2.cloned.1.call-done, f32[16]{0:T(128)S(1)} %copy-done.3), kind=kLoop, calls=%fused_computation | loop fusion | flops 3047424 | bytes 6684736 | tf_op jit(solution)/shard_map/reduce_sum | solution.py:162
  95.0 1.0 multiply_subtract_fusion
  (82 shorter events, 1.3 us)
Async XLA Ops:
  7.2 37.0 %copy-start.1 = (f32[6]{0:T(128)S(1)}, f32[6]{0:T(128)}, u32[]{:S(2)}) copy-start(f32[6]{0:T(128)} %constant.206.clone) | copy-start | bytes 76
  7.2 84.2 %all-gather.2.cloned.1.call-start = ((), (), s32[]{:S(2)}) async-start(), calls=%async_computation | async-start | bytes 6684672 | tf_op jit(solution)/shard_map/all_gather | solution.py:159
  8.9 41.0 %collective-permute-start.1 = (f32[192,128]{0,1:T(8,128)S(1)}, f32[192,128]{0,1:T(8,128)}, u32[]{:S(2)}, u32[]{:S(2)}) collective-permute-start(f32[192,128]{0,1:T(8,128)S(1)} %copy.19), channel_id=1, source_target_pairs={{0,30},{1,31},{2,0},{3,1},{4,2},{5,3},{6,4},{7,5},{8,6},{9,7},{10,... | collective-permute-start | bytes 294920 | tf_op jit(solution)/shard_map/ppermute | solution.py:105
  20.3 29.6 %collective-permute-start = (f32[192,128]{0,1:T(8,128)S(1)}, f32[192,128]{0,1:T(8,128)}, u32[]{:S(2)}, u32[]{:S(2)}) collective-permute-start(f32[192,128]{0,1:T(8,128)S(1)} %copy.19), channel_id=1, source_target_pairs={{0,29},{1,30},{2,31},{3,0},{4,1},{5,2},{6,3},{7,4},{8,5},{9,6},{10... | collective-permute-start | bytes 294920 | tf_op jit(solution)/shard_map/ppermute | solution.py:105
  29.0 20.8 %collective-permute-start.3 = (f32[204,128]{0,1:T(8,128)}, f32[204,128]{0,1:T(8,128)S(1)}, u32[]{:S(2)}, u32[]{:S(2)}) collective-permute-start(f32[204,128]{0,1:T(8,128)} %get-tuple-element.77), channel_id=1, source_target_pairs={{0,1},{1,2},{2,3},{3,4},{4,5},{5,6},{6,7},{7,8},{8,9},{9,10},{10,1... | collective-permute-start | bytes 313352 | tf_op jit(solution)/shard_map/ppermute | solution.py:105
  31.0 18.9 %collective-permute-start.2 = (f32[204,128]{0,1:T(8,128)}, f32[204,128]{0,1:T(8,128)S(1)}, u32[]{:S(2)}, u32[]{:S(2)}) collective-permute-start(f32[204,128]{0,1:T(8,128)} %get-tuple-element.78), channel_id=1, source_target_pairs={{0,31},{1,0},{2,1},{3,2},{4,3},{5,4},{6,5},{7,6},{8,7},{9,8},{10,9... | collective-permute-start | bytes 313352 | tf_op jit(solution)/shard_map/ppermute | solution.py:105
  44.5 24.2 %copy-start = (f32[1,2,6,8,8,128]{5,4,3,2,1,0:T(8,128)S(1)}, f32[1,2,6,8,8,128]{5,4,3,2,1,0:T(8,128)}, u32[]{:S(2)}) copy-start(f32[1,2,6,8,8,128]{5,4,3,2,1,0:T(8,128)} %param.5) | copy-start | bytes 1179652
  47.9 2.8 %copy-start.2 = (s32[128]{0:T(128)S(1)}, s32[128]{0:T(128)}, u32[]{:S(2)}) copy-start(s32[128]{0:T(128)} %iota_add_fusion.1) | copy-start | bytes 1540
  52.5 17.6 %collective-permute-start.6 = (f32[192,128]{1,0:T(8,128)S(1)}, f32[192,128]{1,0:T(8,128)S(1)}, u32[]{:S(2)}, u32[]{:S(2)}) collective-permute-start(f32[192,128]{1,0:T(8,128)S(1)} %bitcast.388), channel_id=1, source_target_pairs={{0,4},{1,5},{2,6},{3,7},{4,8},{5,9},{6,10},{7,11},{8,12},{9,13},{1... | collective-permute-start | bytes 294920 | tf_op jit(solution)/shard_map/ppermute | solution.py:105
  54.7 15.9 %collective-permute-start.5 = (f32[192,128]{1,0:T(8,128)S(1)}, f32[192,128]{1,0:T(8,128)S(1)}, u32[]{:S(2)}, u32[]{:S(2)}) collective-permute-start(f32[192,128]{1,0:T(8,128)S(1)} %bitcast.389), channel_id=1, source_target_pairs={{0,28},{1,29},{2,30},{3,31},{4,0},{5,1},{6,2},{7,3},{8,4},{9,5},{1... | collective-permute-start | bytes 294920 | tf_op jit(solution)/shard_map/ppermute | solution.py:105
  60.5 13.5 %collective-permute-start.4 = (f32[192,128]{1,0:T(8,128)S(1)}, f32[192,128]{1,0:T(8,128)S(1)}, u32[]{:S(2)}, u32[]{:S(2)}) collective-permute-start(f32[192,128]{1,0:T(8,128)S(1)} %bitcast.390), channel_id=1, source_target_pairs={{0,24},{1,25},{2,26},{3,27},{4,28},{5,29},{6,30},{7,31},{8,0},{9,1... | collective-permute-start | bytes 294920 | tf_op jit(solution)/shard_map/ppermute | solution.py:105
  74.0 16.3 %collective-permute-start.7 = (f32[192,128]{1,0:T(8,128)S(1)}, f32[192,128]{1,0:T(8,128)S(1)}, u32[]{:S(2)}, u32[]{:S(2)}) collective-permute-start(f32[192,128]{1,0:T(8,128)S(1)} %bitcast.391), channel_id=1, source_target_pairs={{0,16},{1,17},{2,18},{3,19},{4,20},{5,21},{6,22},{7,23},{8,24},{9,... | collective-permute-start | bytes 294920 | tf_op jit(solution)/shard_map/ppermute | solution.py:105
  84.0 7.4 %copy-start.3 = (f32[16]{0:T(128)S(1)}, f32[16]{0:T(128)}, u32[]{:S(2)}) copy-start(f32[16]{0:T(128)} %fusion.139) | copy-start | bytes 196
Sparse Core Ops, SparseCore 0:
  10.1 58.4 all-gather.1
where the time goes:
time: 103 us
  starting transfers between devices  49.2 us (48%)
  between operations  16.5 us (16%)
  other arithmetic  15.7 us (15%)
  waiting for transfers between devices  10.8 us (10%)
  local copies, waits for them, and re-layouts  10.2 us (10%)
    ppermute x8, starting transfers between devices, shifted(): lax.ppermute(jnp.concatenate(rows, axis=0) if len(rows) > 1 else rows[0],...  49.2 us
    ppermute x8, waiting for transfers between devices, shifted(): lax.ppermute(jnp.concatenate(rows, axis=0) if len(rows) > 1 else rows[0],...  10.1 us
    reduce_sum x1, other arithmetic, per_device(): jnp.sum(weights.reshape((-1,) + (1,) * (piece.ndim - 1)) * piece, axis=0)  3.62 us
    reshape x4, local copies, waits for them, and re-layouts, shifted(): pieces.append(moved[begin:begin + size].reshape(p.shape))  2.51 us
  transfers between devices with their start and end apart: 9, of which 3 were waited for; matrix products, arithmetic and copies ran while one was open for 21% of the time, Pallas kernels for 0%

commit v1 on v0

--- a/solution.py
+++ b/solution.py
@@ -139,23 +139,23 @@
     faces = jnp.stack([fields[1, :, 0:2], fields[0, :, -2:]])
     faces_below, halo_low = shifted([faces, fields[..., -2:]], -1)
     faces_above, halo_high = shifted([faces, fields[..., :2]], 1)
-    near = [faces_below, faces, faces_above] + [shifted([faces], s)[0] for s in (2, 3)]
+    near = [faces_below, faces, faces_above]
     padded = jnp.concatenate([halo_low, fields, halo_high], axis=-1)
-    windows, far_digit, top_digit = [], [], []
+    windows, mid_digit, top_digit = [], [], []
     for t in range(2):
         rotation = jnp.mod(donor_block[0, t, 0] - own_block, total_blocks)
-        low = signed_digit(rotation, 4)
-        rest = jnp.mod((rotation - low) // 4, total_blocks // 4)
-        far_digit.append(signed_digit(rest, 4))
-        top_digit.append(jnp.mod((rest - far_digit[t]) // 4, 2))
+        low = signed_digit(rotation, 2)
+        rest = jnp.mod((rotation - low) // 2, total_blocks // 2)
+        mid_digit.append(signed_digit(rest, 4))
+        top_digit.append(signed_digit(jnp.mod((rest - mid_digit[t]) // 4, 4), 4))
         first = pick([c[t] for c in near], low + 1)
         second = pick([c[t] for c in near], low + 2)
         windows.append(cut_window(first, second, donor_offset[0, t, 0]))
     windows = jnp.stack(windows)
-    far = [shifted([windows], -4)[0], windows] + [shifted([windows], s)[0] for s in (4, 8)]
-    windows = jnp.stack([pick([c[t] for c in far], far_digit[t] + 1) for t in range(2)])
-    top = shifted([windows], 16)[0]
-    rotor_high, stator_low = [jnp.where(top_digit[t] == 1, top[t], windows[t]) for t in range(2)]
+    mid = [shifted([windows], -2)[0], windows] + [shifted([windows], s)[0] for s in (2, 4)]
+    windows = jnp.stack([pick([c[t] for c in mid], mid_digit[t] + 1) for t in range(2)])
+    top = [shifted([windows], -8)[0], windows] + [shifted([windows], s)[0] for s in (8, 16)]
+    rotor_high, stator_low = [pick([c[t] for c in top], top_digit[t] + 1) for t in range(2)]
     piece = lax.all_gather(state, "inst", axis=0, tiled=True)
     sources = jnp.arange(piece.shape[0], dtype=jnp.int32)
     weights = spectral_weights(own_instance, sources, number)

time: 103 us -> 95.4 us (0.926)
  the two profiles are of different devices: /device:TPU:4 before, /device:TPU:104 now
where the time goes in v1:
time: 95.4 us; the launch traced here: 94.9 us
  starting transfers between devices  42.4 us (44%)
  between operations  16.6 us (17%)
  waiting for transfers between devices  13 us (14%)
  other arithmetic  12.8 us (13%)
  local copies, waits for them, and re-layouts  9.52 us (10%)
    ppermute x8, starting transfers between devices, shifted(): lax.ppermute(jnp.concatenate(rows, axis=0) if len(rows) > 1 else rows[0],...  42.4 us
    ppermute x8, waiting for transfers between devices, shifted(): lax.ppermute(jnp.concatenate(rows, axis=0) if len(rows) > 1 else rows[0],...  12.3 us
    reduce_sum x1, other arithmetic, per_device(): jnp.sum(weights.reshape((-1,) + (1,) * (piece.ndim - 1)) * piece, axis=0)  3.62 us
    reshape x4, local copies, waits for them, and re-layouts, shifted(): pieces.append(moved[begin:begin + size].reshape(p.shape))  2.51 us
    sub x5, other arithmetic, flux_divergence(): 0.5 * (take_range(fluxes, 1, length + 1, along) + take_range(fluxes, 2, l...  2.02 us
  transfers between devices with their start and end apart: 9, of which 3 were waited for; matrix products, arithmetic and copies ran while one was open for 19% of the time, Pallas kernels for 0%

profile of v1, /device:TPU:104, one launch (start us, length us, event | category | flops | bytes accessed | tf_op | source)
XLA Modules:
  0.0 94.9 jit_solution(16156642697388142889)
XLA Ops:
  7.2 0.7 all-gather.2.cloned.1.call-update
  7.9 0.8 fusion.163
  8.8 1.3 %fusion.162 = (f32[2,6,8,8,2]{4,3,2,1,0:T(8,128)S(1)}, f32[2,6,8,8,2]{4,3,2,1,0:T(8,128)S(1)}) fusion(f32[2,6,8,8,128]{4,3,2,1,0:T(8,128)} %bitcast.368), kind=kLoop, calls=%fused_computation.372 | loop fusion | bytes 24576 | tf_op jit(solution)/shard_map/slice | solution.py:140
  10.1 0.1 copy.18
  10.2 0.2 reshape.715
  10.4 0.2 reshape.714
  10.6 0.1 copy.27
  10.7 0.1 copy.28
  10.8 0.8 pad_maximum_fusion.17
  11.6 4.2 %collective-permute-start.1 = (f32[204,128]{0,1:T(8,128)}, f32[204,128]{0,1:T(8,128)S(1)}, u32[]{:S(2)}, u32[]{:S(2)}) collective-permute-start(f32[204,128]{0,1:T(8,128)} %get-tuple-element.77), channel_id=1, source_target_pairs={{0,1},{1,2},{2,3},{3,4},{4,5},{5,6},{6,7},{7,8},{8,9},{9,10},{10,1... | collective-permute-start | bytes 313352 | tf_op jit(solution)/shard_map/ppermute | solution.py:105
  15.8 4.0 %collective-permute-start = (f32[204,128]{0,1:T(8,128)}, f32[204,128]{0,1:T(8,128)S(1)}, u32[]{:S(2)}, u32[]{:S(2)}) collective-permute-start(f32[204,128]{0,1:T(8,128)} %get-tuple-element.78), channel_id=1, source_target_pairs={{0,31},{1,0},{2,1},{3,2},{4,3},{5,4},{6,5},{7,6},{8,7},{9,8},{10,9... | collective-permute-start | bytes 313352 | tf_op jit(solution)/shard_map/ppermute | solution.py:105
  19.9 1.4 %fusion.170 = (s32[1,1,1]{1,2,0:T(1,128)}, s32[1,1,1]{1,2,0:T(1,128)}) fusion(s32[1,2,1]{1,2,0:T(1,128)} %param.6), kind=kLoop, calls=%fused_computation.380 | loop fusion | bytes 16 | tf_op jit(solution)/shard_map/slice | solution.py:146
  23.0 1.1 %fusion.118 = f32[2,8,8,128]{3,2,1,0:T(8,128)S(1)} fusion(f32[2,6,8,8,128]{4,3,2,1,0:T(8,128)} %bitcast.369), kind=kLoop, calls=%fused_computation.280 | loop fusion | flops 344064 | bytes 393216 | tf_op jit(solution)/shard_map/mul | solution.py:171
  24.0 1.1 %slice_bitcast_fusion.3 = (f32[6,8,8,128]{3,2,1,0:T(8,128)S(1)}, f32[6,8,8,128]{3,2,1,0:T(8,128)S(1)}) fusion(f32[1,2,6,8,8,128]{5,4,3,2,1,0:T(8,128)} %param.5), kind=kLoop, calls=%fused_computation.99 | loop fusion | bytes 786432 | tf_op jit(solution)/shard_map/squeeze | solution.py:163
  25.2 0.1 rev.13
  25.3 0.1 rev.12
  25.4 0.1 rev.15
  25.6 0.1 rev.14
  25.7 0.1 broadcast_multiply_fusion.6
  25.8 0.1 pad_maximum_fusion.5
  26.0 0.1 fusion.114
  26.1 0.1 fusion.95
  26.1 0.1 fusion.143
  26.2 0.7 fusion.169
  26.9 0.7 iota_add_fusion.1
  27.6 0.1 copy.23
  27.7 0.1 copy.21
  28.3 0.4 fusion.24
  28.6 0.4 fusion.10
  29.0 0.7 iota_add_fusion
  29.7 0.1 select_select_fusion.3
  29.8 0.3 fusion.53
  30.1 0.3 fusion.57
  30.4 6.2 %collective-permute-start.4 = (f32[192,128]{1,0:T(8,128)S(1)}, f32[192,128]{1,0:T(8,128)S(1)}, u32[]{:S(2)}, u32[]{:S(2)}) collective-permute-start(f32[192,128]{1,0:T(8,128)S(1)} %bitcast.388), channel_id=1, source_target_pairs={{0,2},{1,3},{2,4},{3,5},{4,6},{5,7},{6,8},{7,9},{8,10},{9,11},{10,... | collective-permute-start | bytes 294920 | tf_op jit(solution)/shard_map/ppermute | solution.py:105
  36.7 1.9 %collective-permute-start.3 = (f32[192,128]{1,0:T(8,128)S(1)}, f32[192,128]{1,0:T(8,128)S(1)}, u32[]{:S(2)}, u32[]{:S(2)}) collective-permute-start(f32[192,128]{1,0:T(8,128)S(1)} %bitcast.389), channel_id=1, source_target_pairs={{0,30},{1,31},{2,0},{3,1},{4,2},{5,3},{6,4},{7,5},{8,6},{9,7},{10,... | collective-permute-start | bytes 294920 | tf_op jit(solution)/shard_map/ppermute | solution.py:105
  38.6 4.3 %collective-permute-start.2 = (f32[192,128]{1,0:T(8,128)S(1)}, f32[192,128]{1,0:T(8,128)S(1)}, u32[]{:S(2)}, u32[]{:S(2)}) collective-permute-start(f32[192,128]{1,0:T(8,128)S(1)} %bitcast.390), channel_id=1, source_target_pairs={{0,28},{1,29},{2,30},{3,31},{4,0},{5,1},{6,2},{7,3},{8,4},{9,5},{1... | collective-permute-start | bytes 294920 | tf_op jit(solution)/shard_map/ppermute | solution.py:105
  42.9 0.1 slice.849
  43.0 0.1 reshape.704
  43.1 0.1 slice.850
  43.2 0.1 reshape.705
  43.3 1.1 %copy.26 = f32[2,6,8,8,2]{4,3,2,1,0:T(8,128)S(1)} copy(f32[2,6,8,8,2]{1,0,4,3,2:T(2,128)S(1)} %reshape.705) | data formatting | bytes 12288 | tf_op jit(solution)/shard_map/reshape | solution.py:108
  44.5 1.1 %copy.25 = f32[2,6,8,8,2]{4,3,2,1,0:T(8,128)S(1)} copy(f32[2,6,8,8,2]{1,0,4,3,2:T(2,128)S(1)} %reshape.704) | data formatting | bytes 12288 | tf_op jit(solution)/shard_map/reshape | solution.py:108
  45.6 0.4 pad_maximum_fusion
  46.0 0.1 fusion.101
  46.1 0.1 fusion.74
  46.2 0.1 add_divide_fusion.2
  46.4 0.1 add_divide_fusion
  46.5 0.1 subtract_maximum_fusion
  46.6 0.1 subtract_maximum_fusion.2
  46.9 0.1 slice_bitcast_fusion.1
  47.0 0.1 fusion.69
  47.1 0.4 collective-permute-done.3
  47.6 9.2 %collective-permute-start.7 = (f32[192,128]{1,0:T(8,128)S(1)}, f32[192,128]{1,0:T(8,128)S(1)}, u32[]{:S(2)}, u32[]{:S(2)}) collective-permute-start(f32[192,128]{1,0:T(8,128)S(1)} %bitcast.391), channel_id=1, source_target_pairs={{0,8},{1,9},{2,10},{3,11},{4,12},{5,13},{6,14},{7,15},{8,16},{9,17... | collective-permute-start | bytes 294920 | tf_op jit(solution)/shard_map/ppermute | solution.py:105
  56.8 1.9 %collective-permute-start.6 = (f32[192,128]{1,0:T(8,128)S(1)}, f32[192,128]{1,0:T(8,128)S(1)}, u32[]{:S(2)}, u32[]{:S(2)}) collective-permute-start(f32[192,128]{1,0:T(8,128)S(1)} %bitcast.392), channel_id=1, source_target_pairs={{0,24},{1,25},{2,26},{3,27},{4,28},{5,29},{6,30},{7,31},{8,0},{9,1... | collective-permute-start | bytes 294920 | tf_op jit(solution)/shard_map/ppermute | solution.py:105
  58.7 10.6 %collective-permute-start.5 = (f32[192,128]{1,0:T(8,128)S(1)}, f32[192,128]{1,0:T(8,128)S(1)}, u32[]{:S(2)}, u32[]{:S(2)}) collective-permute-start(f32[192,128]{1,0:T(8,128)S(1)} %bitcast.393), channel_id=1, source_target_pairs={{0,16},{1,17},{2,18},{3,19},{4,20},{5,21},{6,22},{7,23},{8,24},{9,... | collective-permute-start | bytes 294920 | tf_op jit(solution)/shard_map/ppermute | solution.py:105
  69.3 1.1 %fusion.3 = (f32[6,8,8,129]{3,2,1,0:T(8,128)S(1)}, f32[6,8,8,129]{3,2,1,0:T(8,128)S(1)}) fusion(f32[6,8,8,132]{3,2,1,0:T(8,128)S(1)} %get-tuple-element.60, f32[6,8,8,132]{3,2,1,0:T(8,128)S(1)} %constant_dynamic-update-slice_fusion.30, f32[8,8,129]{2,1,0:T(8,128)S(1)} %get-tuple-element.44, f32[8,8,129]{2,1,0:T(8,128)S(1)} %get-tuple-element.45, ...), kind=kLoop, calls=%fused_computation.6 | loop fusion | flops 1287936 | bytes 2972160 | tf_op jit(solution)/shard_map/sub | solution.py:69
  70.4 5.6 %collective-permute-done.6 = f32[192,128]{1,0:T(8,128)S(1)} collective-permute-done((f32[192,128]{1,0:T(8,128)S(1)}, f32[192,128]{1,0:T(8,128)S(1)}, u32[]{:S(2)}, u32[]{:S(2)}) %collective-permute-start.6) | collective-permute-done | bytes 98336 | tf_op jit(solution)/shard_map/ppermute | solution.py:105
  76.0 6.3 %collective-permute-done.5 = f32[192,128]{1,0:T(8,128)S(1)} collective-permute-done((f32[192,128]{1,0:T(8,128)S(1)}, f32[192,128]{1,0:T(8,128)S(1)}, u32[]{:S(2)}, u32[]{:S(2)}) %collective-permute-start.5) | collective-permute-done | bytes 98336 | tf_op jit(solution)/shard_map/ppermute | solution.py:105
  82.9 0.1 fusion.42
  83.0 0.1 fusion.36
  83.1 0.1 fusion.51
  83.3 0.1 fusion.48
  83.4 3.6 %multiply_reduce_fusion = f32[2,6,8,8,128]{4,3,2,1,0:T(8,128)S(1)} fusion(f32[16,2,6,8,8,128]{5,4,3,2,1,0:T(8,128)} %all-gather.2.cloned.1.call-done, f32[16]{0:T(128)S(1)} %fusion.143), kind=kLoop, calls=%fused_computation | loop fusion | flops 3047424 | bytes 6684736 | tf_op jit(solution)/shard_map/reduce_sum | solution.py:162
  87.0 1.0 %multiply_subtract_fusion = (f32[1,2,6,8,8,128]{5,4,3,2,1,0:T(8,128)}, f32[1,2,6,8,8,128]{5,4,3,2,1,0:T(8,128)}) fusion(f32[1,2,6,8,8,128]{5,4,3,2,1,0:T(8,128)S(1)} %copy-done, f32[2,8,8,128]{3,2,1,0:T(8,128)S(1)} %fusion.118, f32[2,6,8,8,128]{4,3,2,1,0:T(8,128)S(1)} %multiply_reduce_fusion, f32[1,1,6,8,8,128]{5,4,3,2,1,0:T(8,128)S(1)} %fusion.48, ...), kind=kLoop, calls=%fused_computation.51 | loop fusion | flops 393216 | bytes 2031616 | tf_op jit(solution)/shard_map/sub | solution.py:171
  (80 shorter events, 1.2 us)
Async XLA Ops:
  7.2 18.5 %copy-start.2 = (f32[6]{0:T(128)S(1)}, f32[6]{0:T(128)}, u32[]{:S(2)}) copy-start(f32[6]{0:T(128)} %constant.213.clone) | copy-start | bytes 76
  7.2 19.0 %copy-start.1 = (s32[1,2,1]{1,2,0:T(1,128)S(1)}, s32[1,2,1]{1,2,0:T(1,128)}, u32[]{:S(2)}) copy-start(s32[1,2,1]{1,2,0:T(1,128)} %param.7) | copy-start | bytes 28
  7.2 76.2 %all-gather.2.cloned.1.call-start = ((), (), s32[]{:S(2)}) async-start(), calls=%async_computation | async-start | bytes 6684672 | tf_op jit(solution)/shard_map/all_gather | solution.py:159
  11.6 18.1 %collective-permute-start.1 = (f32[204,128]{0,1:T(8,128)}, f32[204,128]{0,1:T(8,128)S(1)}, u32[]{:S(2)}, u32[]{:S(2)}) collective-permute-start(f32[204,128]{0,1:T(8,128)} %get-tuple-element.77), channel_id=1, source_target_pairs={{0,1},{1,2},{2,3},{3,4},{4,5},{5,6},{6,7},{7,8},{8,9},{9,10},{10,1... | collective-permute-start | bytes 313352 | tf_op jit(solution)/shard_map/ppermute | solution.py:105
  15.8 13.9 %collective-permute-start = (f32[204,128]{0,1:T(8,128)}, f32[204,128]{0,1:T(8,128)S(1)}, u32[]{:S(2)}, u32[]{:S(2)}) collective-permute-start(f32[204,128]{0,1:T(8,128)} %get-tuple-element.78), channel_id=1, source_target_pairs={{0,31},{1,0},{2,1},{3,2},{4,3},{5,4},{6,5},{7,6},{8,7},{9,8},{10,9... | collective-permute-start | bytes 313352 | tf_op jit(solution)/shard_map/ppermute | solution.py:105
  26.0 19.6 %copy-start = (f32[1,2,6,8,8,128]{5,4,3,2,1,0:T(8,128)S(1)}, f32[1,2,6,8,8,128]{5,4,3,2,1,0:T(8,128)}, u32[]{:S(2)}) copy-start(f32[1,2,6,8,8,128]{5,4,3,2,1,0:T(8,128)} %param.5) | copy-start | bytes 1179652
  30.4 16.7 %collective-permute-start.4 = (f32[192,128]{1,0:T(8,128)S(1)}, f32[192,128]{1,0:T(8,128)S(1)}, u32[]{:S(2)}, u32[]{:S(2)}) collective-permute-start(f32[192,128]{1,0:T(8,128)S(1)} %bitcast.388), channel_id=1, source_target_pairs={{0,2},{1,3},{2,4},{3,5},{4,6},{5,7},{6,8},{7,9},{8,10},{9,11},{10,... | collective-permute-start | bytes 294920 | tf_op jit(solution)/shard_map/ppermute | solution.py:105
  36.7 10.8 %collective-permute-start.3 = (f32[192,128]{1,0:T(8,128)S(1)}, f32[192,128]{1,0:T(8,128)S(1)}, u32[]{:S(2)}, u32[]{:S(2)}) collective-permute-start(f32[192,128]{1,0:T(8,128)S(1)} %bitcast.389), channel_id=1, source_target_pairs={{0,30},{1,31},{2,0},{3,1},{4,2},{5,3},{6,4},{7,5},{8,6},{9,7},{10,... | collective-permute-start | bytes 294920 | tf_op jit(solution)/shard_map/ppermute | solution.py:105
  38.6 8.9 %collective-permute-start.2 = (f32[192,128]{1,0:T(8,128)S(1)}, f32[192,128]{1,0:T(8,128)S(1)}, u32[]{:S(2)}, u32[]{:S(2)}) collective-permute-start(f32[192,128]{1,0:T(8,128)S(1)} %bitcast.390), channel_id=1, source_target_pairs={{0,28},{1,29},{2,30},{3,31},{4,0},{5,1},{6,2},{7,3},{8,4},{9,5},{1... | collective-permute-start | bytes 294920 | tf_op jit(solution)/shard_map/ppermute | solution.py:105
  47.6 22.8 %collective-permute-start.7 = (f32[192,128]{1,0:T(8,128)S(1)}, f32[192,128]{1,0:T(8,128)S(1)}, u32[]{:S(2)}, u32[]{:S(2)}) collective-permute-start(f32[192,128]{1,0:T(8,128)S(1)} %bitcast.391), channel_id=1, source_target_pairs={{0,8},{1,9},{2,10},{3,11},{4,12},{5,13},{6,14},{7,15},{8,16},{9,17... | collective-permute-start | bytes 294920 | tf_op jit(solution)/shard_map/ppermute | solution.py:105
  56.8 19.3 %collective-permute-start.6 = (f32[192,128]{1,0:T(8,128)S(1)}, f32[192,128]{1,0:T(8,128)S(1)}, u32[]{:S(2)}, u32[]{:S(2)}) collective-permute-start(f32[192,128]{1,0:T(8,128)S(1)} %bitcast.392), channel_id=1, source_target_pairs={{0,24},{1,25},{2,26},{3,27},{4,28},{5,29},{6,30},{7,31},{8,0},{9,1... | collective-permute-start | bytes 294920 | tf_op jit(solution)/shard_map/ppermute | solution.py:105
  58.7 23.6 %collective-permute-start.5 = (f32[192,128]{1,0:T(8,128)S(1)}, f32[192,128]{1,0:T(8,128)S(1)}, u32[]{:S(2)}, u32[]{:S(2)}) collective-permute-start(f32[192,128]{1,0:T(8,128)S(1)} %bitcast.393), channel_id=1, source_target_pairs={{0,16},{1,17},{2,18},{3,19},{4,20},{5,21},{6,22},{7,23},{8,24},{9,... | collective-permute-start | bytes 294920 | tf_op jit(solution)/shard_map/ppermute | solution.py:105
Sparse Core Ops, SparseCore 0:
  10.1 53.2 all-gather.1

commit v2 on v1

--- a/solution.py
+++ b/solution.py
@@ -8,7 +8,6 @@
 fourth_coef = 1.0 / 32.0
 courant = 0.8
 frequency = 0.5
-highest = lax.Precision.HIGHEST
 
 
 def spectral_weights(target, source, number):
@@ -111,19 +110,7 @@
 
 
 def pick(candidates, index):
-    chosen = candidates[0]
-    for k in range(1, len(candidates)):
-        chosen = jnp.where(index == k, candidates[k], chosen)
-    return chosen
-
-
-def cut_window(first, second, offset):
-    width = first.shape[-1]
-    joined = jnp.concatenate([first, second], axis=-1).reshape(-1, 2 * width)
-    rows = lax.broadcasted_iota(jnp.int32, (2 * width, width), 0)
-    cols = lax.broadcasted_iota(jnp.int32, (2 * width, width), 1)
-    selection = (rows == cols + offset).astype(jnp.float32)
-    return jnp.dot(joined, selection, precision=highest).reshape(first.shape)
+    return lax.dynamic_index_in_dim(jnp.stack(candidates), index, 0, keepdims=False)
 
 
 def signed_digit(value, radix):
@@ -136,6 +123,7 @@
     own_instance = lax.axis_index("inst")
     own_block = lax.axis_index("blk")
     fields = state[0]
+    width = fields.shape[-1]
     faces = jnp.stack([fields[1, :, 0:2], fields[0, :, -2:]])
     faces_below, halo_low = shifted([faces, fields[..., -2:]], -1)
     faces_above, halo_high = shifted([faces, fields[..., :2]], 1)
@@ -150,12 +138,13 @@
         top_digit.append(signed_digit(jnp.mod((rest - mid_digit[t]) // 4, 4), 4))
         first = pick([c[t] for c in near], low + 1)
         second = pick([c[t] for c in near], low + 2)
-        windows.append(cut_window(first, second, donor_offset[0, t, 0]))
+        joined = jnp.concatenate([first, second], axis=-1)
+        windows.append(lax.dynamic_slice_in_dim(joined, donor_offset[0, t, 0], width, axis=-1))
     windows = jnp.stack(windows)
-    mid = [shifted([windows], -2)[0], windows] + [shifted([windows], s)[0] for s in (2, 4)]
-    windows = jnp.stack([pick([c[t] for c in mid], mid_digit[t] + 1) for t in range(2)])
-    top = [shifted([windows], -8)[0], windows] + [shifted([windows], s)[0] for s in (8, 16)]
-    rotor_high, stator_low = [pick([c[t] for c in top], top_digit[t] + 1) for t in range(2)]
+    far = [shifted([windows], -8)[0], windows] + [shifted([windows], s)[0] for s in (8, 16)]
+    windows = jnp.stack([pick([c[t] for c in far], top_digit[t] + 1) for t in range(2)])
+    near_last = [shifted([windows], -2)[0], windows] + [shifted([windows], s)[0] for s in (2, 4)]
+    rotor_high, stator_low = [pick([c[t] for c in near_last], mid_digit[t] + 1) for t in range(2)]
     piece = lax.all_gather(state, "inst", axis=0, tiled=True)
     sources = jnp.arange(piece.shape[0], dtype=jnp.int32)
     weights = spectral_weights(own_instance, sources, number)

time: 95.4 us -> 97.6 us (1.023)
  the two profiles are of different devices: /device:TPU:104 before, /device:TPU:2 now
where the time goes in v2:
time: 97.6 us; the launch traced here: 97 us
  starting transfers between devices  46.4 us (48%)
  between operations  20.6 us (21%)
  other arithmetic  11.5 us (12%)
  local copies, waits for them, and re-layouts  10.6 us (11%)
  waiting for transfers between devices  8.01 us (8%)
    ppermute x8, starting transfers between devices, shifted(): lax.ppermute(jnp.concatenate(rows, axis=0) if len(rows) > 1 else rows[0],...  46.3 us
    ppermute x8, waiting for transfers between devices, shifted(): lax.ppermute(jnp.concatenate(rows, axis=0) if len(rows) > 1 else rows[0],...  7.31 us
    reduce_sum x1, other arithmetic, per_device(): jnp.sum(weights.reshape((-1,) + (1,) * (piece.ndim - 1)) * piece, axis=0)  3.62 us
    reshape x4, local copies, waits for them, and re-layouts, shifted(): pieces.append(moved[begin:begin + size].reshape(p.shape))  2.51 us
    sub x5, other arithmetic, flux_divergence(): 0.5 * (take_range(fluxes, 1, length + 1, along) + take_range(fluxes, 2, l...  2.02 us
  transfers between devices with their start and end apart: 9, of which 3 were waited for; matrix products, arithmetic and copies ran while one was open for 18% of the time, Pallas kernels for 0%

profile of v2, /device:TPU:2, one launch (start us, length us, event | category | flops | bytes accessed | tf_op | source)
XLA Modules:
  0.0 97.0 jit_solution(5538268844748878727)
XLA Ops:
  7.2 0.7 all-gather.2.cloned.1.call-update
  7.9 0.8 fusion.165
  8.7 1.3 %fusion.164 = (f32[2,6,8,8,2]{4,3,2,1,0:T(8,128)S(1)}, f32[2,6,8,8,2]{4,3,2,1,0:T(8,128)S(1)}) fusion(f32[2,6,8,8,128]{4,3,2,1,0:T(8,128)} %bitcast.388), kind=kLoop, calls=%fused_computation.388 | loop fusion | bytes 24576 | tf_op jit(solution)/shard_map/slice | solution.py:128
  10.1 0.1 copy.18
  10.2 0.2 reshape.590
  10.4 0.2 reshape.591
  10.6 0.1 copy.28
  10.7 0.1 copy.27
  10.8 0.7 pad_maximum_fusion.18
  11.6 5.1 %collective-permute-start = (f32[204,128]{0,1:T(8,128)}, f32[204,128]{0,1:T(8,128)S(1)}, u32[]{:S(2)}, u32[]{:S(2)}) collective-permute-start(f32[204,128]{0,1:T(8,128)} %get-tuple-element.79), channel_id=1, source_target_pairs={{0,1},{1,2},{2,3},{3,4},{4,5},{5,6},{6,7},{7,8},{8,9},{9,10},{10,1... | collective-permute-start | bytes 313352 | tf_op jit(solution)/shard_map/ppermute | solution.py:104
  16.7 10.9 %collective-permute-start.1 = (f32[204,128]{0,1:T(8,128)S(1)}, f32[204,128]{0,1:T(8,128)S(1)}, u32[]{:S(2)}, u32[]{:S(2)}) collective-permute-start(f32[204,128]{0,1:T(8,128)S(1)} %get-tuple-element.80), channel_id=1, source_target_pairs={{0,31},{1,0},{2,1},{3,2},{4,3},{5,4},{6,5},{7,6},{8,7},{9,8},{10,9... | collective-permute-start | bytes 313352 | tf_op jit(solution)/shard_map/ppermute | solution.py:104
  27.5 1.4 %fusion.176 = (s32[1,1,1]{1,2,0:T(1,128)}, s32[1,1,1]{1,2,0:T(1,128)}) fusion(s32[1,2,1]{1,2,0:T(1,128)} %param.6), kind=kLoop, calls=%fused_computation.400 | loop fusion | bytes 16 | tf_op jit(solution)/shard_map/slice | solution.py:134
  30.5 1.4 %fusion.177 = (s32[1,1,1]{1,2,0:T(1,128)}, s32[1,1,1]{1,2,0:T(1,128)}) fusion(s32[1,2,1]{1,2,0:T(1,128)} %param.7), kind=kLoop, calls=%fused_computation.401 | loop fusion | bytes 16 | tf_op jit(solution)/shard_map/slice | solution.py:142
  34.6 1.1 %fusion.108 = f32[2,8,8,128]{3,2,1,0:T(8,128)S(1)} fusion(f32[2,6,8,8,128]{4,3,2,1,0:T(8,128)} %bitcast.389), kind=kLoop, calls=%fused_computation.286 | loop fusion | flops 344064 | bytes 393216 | tf_op jit(solution)/shard_map/mul | solution.py:160
  35.6 1.1 %slice_bitcast_fusion.3 = (f32[6,8,8,128]{3,2,1,0:T(8,128)S(1)}, f32[6,8,8,128]{3,2,1,0:T(8,128)S(1)}) fusion(f32[1,2,6,8,8,128]{5,4,3,2,1,0:T(8,128)} %param.5), kind=kLoop, calls=%fused_computation.115 | loop fusion | bytes 786432 | tf_op jit(solution)/shard_map/squeeze | solution.py:152
  36.8 0.1 rev.13
  36.9 0.1 rev.12
  37.0 0.1 rev.15
  37.2 0.1 rev.14
  37.3 0.1 broadcast_multiply_fusion.6
  37.4 0.1 pad_maximum_fusion.5
  37.6 0.1 fusion.106
  37.7 0.1 fusion.87
  39.6 0.4 fusion.24
  40.0 0.4 fusion.10
  40.4 0.1 fusion.168
  40.5 0.1 copy.19
  40.6 0.1 copy.23
  40.7 0.1 fusion.169
  40.8 0.1 copy.22
  40.8 0.1 copy.24
  41.0 0.1 fusion.112
  41.1 0.1 fusion.110
  41.2 9.3 %collective-permute-start.4 = (f32[192,128]{1,0:T(8,128)S(1)}, f32[192,128]{1,0:T(8,128)S(1)}, u32[]{:S(2)}, u32[]{:S(2)}) collective-permute-start(f32[192,128]{1,0:T(8,128)S(1)} %bitcast.408), channel_id=1, source_target_pairs={{0,16},{1,17},{2,18},{3,19},{4,20},{5,21},{6,22},{7,23},{8,24},{9,... | collective-permute-start | bytes 294920 | tf_op jit(solution)/shard_map/ppermute | solution.py:104
  50.5 1.9 %collective-permute-start.3 = (f32[192,128]{1,0:T(8,128)S(1)}, f32[192,128]{1,0:T(8,128)S(1)}, u32[]{:S(2)}, u32[]{:S(2)}) collective-permute-start(f32[192,128]{1,0:T(8,128)S(1)} %bitcast.409), channel_id=1, source_target_pairs={{0,24},{1,25},{2,26},{3,27},{4,28},{5,29},{6,30},{7,31},{8,0},{9,1... | collective-permute-start | bytes 294920 | tf_op jit(solution)/shard_map/ppermute | solution.py:104
  52.5 7.8 %collective-permute-start.2 = (f32[192,128]{1,0:T(8,128)S(1)}, f32[192,128]{1,0:T(8,128)S(1)}, u32[]{:S(2)}, u32[]{:S(2)}) collective-permute-start(f32[192,128]{1,0:T(8,128)S(1)} %bitcast.410), channel_id=1, source_target_pairs={{0,8},{1,9},{2,10},{3,11},{4,12},{5,13},{6,14},{7,15},{8,16},{9,17... | collective-permute-start | bytes 294920 | tf_op jit(solution)/shard_map/ppermute | solution.py:104
  60.3 0.1 slice.897
  60.4 0.1 reshape.588
  60.5 0.1 slice.898
  60.6 0.1 reshape.589
  60.7 1.1 %copy.26 = f32[2,6,8,8,2]{4,3,2,1,0:T(8,128)S(1)} copy(f32[2,6,8,8,2]{1,0,4,3,2:T(2,128)S(1)} %reshape.589) | data formatting | bytes 12288 | tf_op jit(solution)/shard_map/reshape | solution.py:107
  61.9 1.1 %copy.25 = f32[2,6,8,8,2]{4,3,2,1,0:T(8,128)S(1)} copy(f32[2,6,8,8,2]{1,0,4,3,2:T(2,128)S(1)} %reshape.588) | data formatting | bytes 12288 | tf_op jit(solution)/shard_map/reshape | solution.py:107
  63.0 0.4 pad_maximum_fusion
  63.4 0.1 fusion.93
  63.5 0.1 fusion.66
  63.6 0.1 add_divide_fusion.2
  63.8 0.1 add_divide_fusion
  63.9 0.1 subtract_maximum_fusion
  64.0 0.1 subtract_maximum_fusion.2
  64.3 0.1 slice_bitcast_fusion.1
  64.4 0.1 fusion.61
  64.5 2.1 %collective-permute-done.3 = f32[192,128]{1,0:T(8,128)S(1)} collective-permute-done((f32[192,128]{1,0:T(8,128)S(1)}, f32[192,128]{1,0:T(8,128)S(1)}, u32[]{:S(2)}, u32[]{:S(2)}) %collective-permute-start.3) | collective-permute-done | bytes 98336 | tf_op jit(solution)/shard_map/ppermute | solution.py:104
  66.7 5.5 %collective-permute-start.7 = (f32[192,128]{1,0:T(8,128)S(1)}, f32[192,128]{1,0:T(8,128)S(1)}, u32[]{:S(2)}, u32[]{:S(2)}) collective-permute-start(f32[192,128]{1,0:T(8,128)S(1)} %bitcast.411), channel_id=1, source_target_pairs={{0,28},{1,29},{2,30},{3,31},{4,0},{5,1},{6,2},{7,3},{8,4},{9,5},{1... | collective-permute-start | bytes 294920 | tf_op jit(solution)/shard_map/ppermute | solution.py:104
  72.2 1.1 %fusion.3 = (f32[6,8,8,129]{3,2,1,0:T(8,128)S(1)}, f32[6,8,8,129]{3,2,1,0:T(8,128)S(1)}) fusion(f32[6,8,8,132]{3,2,1,0:T(8,128)S(1)} %get-tuple-element.60, f32[6,8,8,132]{3,2,1,0:T(8,128)S(1)} %constant_dynamic-update-slice_fusion.30, f32[8,8,129]{2,1,0:T(8,128)S(1)} %get-tuple-element.44, f32[8,8,129]{2,1,0:T(8,128)S(1)} %get-tuple-element.45, ...), kind=kLoop, calls=%fused_computation.6 | loop fusion | flops 1287936 | bytes 2972160 | tf_op jit(solution)/shard_map/sub | solution.py:68
  73.3 3.4 %collective-permute-start.6 = (f32[192,128]{1,0:T(8,128)S(1)}, f32[192,128]{1,0:T(8,128)S(1)}, u32[]{:S(2)}, u32[]{:S(2)}) collective-permute-start(f32[192,128]{1,0:T(8,128)S(1)} %bitcast.412), channel_id=1, source_target_pairs={{0,30},{1,31},{2,0},{3,1},{4,2},{5,3},{6,4},{7,5},{8,6},{9,7},{10,... | collective-permute-start | bytes 294920 | tf_op jit(solution)/shard_map/ppermute | solution.py:104
  76.7 2.5 %collective-permute-start.5 = (f32[192,128]{1,0:T(8,128)S(1)}, f32[192,128]{1,0:T(8,128)S(1)}, u32[]{:S(2)}, u32[]{:S(2)}) collective-permute-start(f32[192,128]{1,0:T(8,128)S(1)} %bitcast.413), channel_id=1, source_target_pairs={{0,2},{1,3},{2,4},{3,5},{4,6},{5,7},{6,8},{7,9},{8,10},{9,11},{10,... | collective-permute-start | bytes 294920 | tf_op jit(solution)/shard_map/ppermute | solution.py:104
  79.2 0.6 collective-permute-done.6
  79.8 4.6 %collective-permute-done.5 = f32[192,128]{1,0:T(8,128)S(1)} collective-permute-done((f32[192,128]{1,0:T(8,128)S(1)}, f32[192,128]{1,0:T(8,128)S(1)}, u32[]{:S(2)}, u32[]{:S(2)}) %collective-permute-start.5) | collective-permute-done | bytes 98336 | tf_op jit(solution)/shard_map/ppermute | solution.py:104
  85.1 0.1 fusion.42
  85.2 0.1 fusion.36
  85.3 0.1 fusion.51
  85.4 0.1 fusion.48
  85.6 3.6 %multiply_reduce_fusion = f32[2,6,8,8,128]{4,3,2,1,0:T(8,128)S(1)} fusion(f32[16,2,6,8,8,128]{5,4,3,2,1,0:T(8,128)} %all-gather.2.cloned.1.call-done, f32[16]{0:T(128)S(1)} %fusion.147), kind=kLoop, calls=%fused_computation | loop fusion | flops 3047424 | bytes 6684736 | tf_op jit(solution)/shard_map/reduce_sum | solution.py:151
  89.2 1.0 %multiply_subtract_fusion = (f32[1,2,6,8,8,128]{5,4,3,2,1,0:T(8,128)}, f32[1,2,6,8,8,128]{5,4,3,2,1,0:T(8,128)}) fusion(f32[1,2,6,8,8,128]{5,4,3,2,1,0:T(8,128)S(1)} %copy-done, f32[2,8,8,128]{3,2,1,0:T(8,128)S(1)} %fusion.108, f32[2,6,8,8,128]{4,3,2,1,0:T(8,128)S(1)} %multiply_reduce_fusion, f32[1,1,6,8,8,128]{5,4,3,2,1,0:T(8,128)S(1)} %fusion.48, ...), kind=kLoop, calls=%fused_computation.51 | loop fusion | flops 393216 | bytes 2031616 | tf_op jit(solution)/shard_map/sub | solution.py:160
  (86 shorter events, 1.4 us)
Async XLA Ops:
  7.2 30.1 %copy-start.1 = (f32[6]{0:T(128)S(1)}, f32[6]{0:T(128)}, u32[]{:S(2)}) copy-start(f32[6]{0:T(128)} %constant.251.clone) | copy-start | bytes 76
  7.2 78.4 %all-gather.2.cloned.1.call-start = ((), (), s32[]{:S(2)}) async-start(), calls=%async_computation | async-start | bytes 6684672 | tf_op jit(solution)/shard_map/all_gather | solution.py:148
  11.6 28.8 %collective-permute-start = (f32[204,128]{0,1:T(8,128)}, f32[204,128]{0,1:T(8,128)S(1)}, u32[]{:S(2)}, u32[]{:S(2)}) collective-permute-start(f32[204,128]{0,1:T(8,128)} %get-tuple-element.79), channel_id=1, source_target_pairs={{0,1},{1,2},{2,3},{3,4},{4,5},{5,6},{6,7},{7,8},{8,9},{9,10},{10,1... | collective-permute-start | bytes 313352 | tf_op jit(solution)/shard_map/ppermute | solution.py:104
  16.7 24.0 %collective-permute-start.1 = (f32[204,128]{0,1:T(8,128)S(1)}, f32[204,128]{0,1:T(8,128)S(1)}, u32[]{:S(2)}, u32[]{:S(2)}) collective-permute-start(f32[204,128]{0,1:T(8,128)S(1)} %get-tuple-element.80), channel_id=1, source_target_pairs={{0,31},{1,0},{2,1},{3,2},{4,3},{5,4},{6,5},{7,6},{8,7},{9,8},{10,9... | collective-permute-start | bytes 313352 | tf_op jit(solution)/shard_map/ppermute | solution.py:104
  37.7 25.3 %copy-start = (f32[1,2,6,8,8,128]{5,4,3,2,1,0:T(8,128)S(1)}, f32[1,2,6,8,8,128]{5,4,3,2,1,0:T(8,128)}, u32[]{:S(2)}) copy-start(f32[1,2,6,8,8,128]{5,4,3,2,1,0:T(8,128)} %param.5) | copy-start | bytes 1179652
  41.2 23.2 %collective-permute-start.4 = (f32[192,128]{1,0:T(8,128)S(1)}, f32[192,128]{1,0:T(8,128)S(1)}, u32[]{:S(2)}, u32[]{:S(2)}) collective-permute-start(f32[192,128]{1,0:T(8,128)S(1)} %bitcast.408), channel_id=1, source_target_pairs={{0,16},{1,17},{2,18},{3,19},{4,20},{5,21},{6,22},{7,23},{8,24},{9,... | collective-permute-start | bytes 294920 | tf_op jit(solution)/shard_map/ppermute | solution.py:104
  50.5 16.0 %collective-permute-start.3 = (f32[192,128]{1,0:T(8,128)S(1)}, f32[192,128]{1,0:T(8,128)S(1)}, u32[]{:S(2)}, u32[]{:S(2)}) collective-permute-start(f32[192,128]{1,0:T(8,128)S(1)} %bitcast.409), channel_id=1, source_target_pairs={{0,24},{1,25},{2,26},{3,27},{4,28},{5,29},{6,30},{7,31},{8,0},{9,1... | collective-permute-start | bytes 294920 | tf_op jit(solution)/shard_map/ppermute | solution.py:104
  52.5 14.1 %collective-permute-start.2 = (f32[192,128]{1,0:T(8,128)S(1)}, f32[192,128]{1,0:T(8,128)S(1)}, u32[]{:S(2)}, u32[]{:S(2)}) collective-permute-start(f32[192,128]{1,0:T(8,128)S(1)} %bitcast.410), channel_id=1, source_target_pairs={{0,8},{1,9},{2,10},{3,11},{4,12},{5,13},{6,14},{7,15},{8,16},{9,17... | collective-permute-start | bytes 294920 | tf_op jit(solution)/shard_map/ppermute | solution.py:104
  66.7 12.5 %collective-permute-start.7 = (f32[192,128]{1,0:T(8,128)S(1)}, f32[192,128]{1,0:T(8,128)S(1)}, u32[]{:S(2)}, u32[]{:S(2)}) collective-permute-start(f32[192,128]{1,0:T(8,128)S(1)} %bitcast.411), channel_id=1, source_target_pairs={{0,28},{1,29},{2,30},{3,31},{4,0},{5,1},{6,2},{7,3},{8,4},{9,5},{1... | collective-permute-start | bytes 294920 | tf_op jit(solution)/shard_map/ppermute | solution.py:104
  73.3 6.5 %collective-permute-start.6 = (f32[192,128]{1,0:T(8,128)S(1)}, f32[192,128]{1,0:T(8,128)S(1)}, u32[]{:S(2)}, u32[]{:S(2)}) collective-permute-start(f32[192,128]{1,0:T(8,128)S(1)} %bitcast.412), channel_id=1, source_target_pairs={{0,30},{1,31},{2,0},{3,1},{4,2},{5,3},{6,4},{7,5},{8,6},{9,7},{10,... | collective-permute-start | bytes 294920 | tf_op jit(solution)/shard_map/ppermute | solution.py:104
  76.7 7.7 %collective-permute-start.5 = (f32[192,128]{1,0:T(8,128)S(1)}, f32[192,128]{1,0:T(8,128)S(1)}, u32[]{:S(2)}, u32[]{:S(2)}) collective-permute-start(f32[192,128]{1,0:T(8,128)S(1)} %bitcast.413), channel_id=1, source_target_pairs={{0,2},{1,3},{2,4},{3,5},{4,6},{5,7},{6,8},{7,9},{8,10},{9,11},{10,... | collective-permute-start | bytes 294920 | tf_op jit(solution)/shard_map/ppermute | solution.py:104
Sparse Core Ops, SparseCore 0:
  10.1 54.2 all-gather.1

commit v3 on v2

--- a/solution.py
+++ b/solution.py
@@ -136,15 +136,16 @@
         rest = jnp.mod((rotation - low) // 2, total_blocks // 2)
         mid_digit.append(signed_digit(rest, 4))
         top_digit.append(signed_digit(jnp.mod((rest - mid_digit[t]) // 4, 4), 4))
+        offset = donor_offset[0, t, 0] + 0 * rotation
         first = pick([c[t] for c in near], low + 1)
         second = pick([c[t] for c in near], low + 2)
         joined = jnp.concatenate([first, second], axis=-1)
-        windows.append(lax.dynamic_slice_in_dim(joined, donor_offset[0, t, 0], width, axis=-1))
+        windows.append(lax.dynamic_slice_in_dim(joined, offset, width, axis=-1))
     windows = jnp.stack(windows)
-    far = [shifted([windows], -8)[0], windows] + [shifted([windows], s)[0] for s in (8, 16)]
-    windows = jnp.stack([pick([c[t] for c in far], top_digit[t] + 1) for t in range(2)])
-    near_last = [shifted([windows], -2)[0], windows] + [shifted([windows], s)[0] for s in (2, 4)]
-    rotor_high, stator_low = [pick([c[t] for c in near_last], mid_digit[t] + 1) for t in range(2)]
+    mid = [shifted([windows], -2)[0], windows] + [shifted([windows], s)[0] for s in (2, 4)]
+    windows = jnp.stack([pick([c[t] for c in mid], mid_digit[t] + 1) for t in range(2)])
+    top = [shifted([windows], -8)[0], windows] + [shifted([windows], s)[0] for s in (8, 16)]
+    rotor_high, stator_low = [pick([c[t] for c in top], top_digit[t] + 1) for t in range(2)]
     piece = lax.all_gather(state, "inst", axis=0, tiled=True)
     sources = jnp.arange(piece.shape[0], dtype=jnp.int32)
     weights = spectral_weights(own_instance, sources, number)

time: 97.6 us -> 97.1 us (level)
  the two profiles are of different devices: /device:TPU:2 before, /device:TPU:1 now
where the time goes in v3:
time: 97.1 us; the launch traced here: 96.5 us
  starting transfers between devices  41.6 us (43%)
  between operations  20.6 us (21%)
  waiting for transfers between devices  12.2 us (13%)
  other arithmetic  11.5 us (12%)
  local copies, waits for them, and re-layouts  10.6 us (11%)
    ppermute x8, starting transfers between devices, shifted(): lax.ppermute(jnp.concatenate(rows, axis=0) if len(rows) > 1 else rows[0],...  41.6 us
    ppermute x8, waiting for transfers between devices, shifted(): lax.ppermute(jnp.concatenate(rows, axis=0) if len(rows) > 1 else rows[0],...  11.5 us
    reduce_sum x1, other arithmetic, per_device(): jnp.sum(weights.reshape((-1,) + (1,) * (piece.ndim - 1)) * piece, axis=0)  3.62 us
    reshape x4, local copies, waits for them, and re-layouts, shifted(): pieces.append(moved[begin:begin + size].reshape(p.shape))  2.51 us
    sub x5, other arithmetic, flux_divergence(): 0.5 * (take_range(fluxes, 1, length + 1, along) + take_range(fluxes, 2, l...  2.02 us
  transfers between devices with their start and end apart: 9, of which 1 were waited for; matrix products, arithmetic and copies ran while one was open for 18% of the time, Pallas kernels for 0%

profile of v3, /device:TPU:1, one launch (start us, length us, event | category | flops | bytes accessed | tf_op | source)
XLA Modules:
  0.0 96.5 jit_solution(10439591371321669352)
XLA Ops:
  7.2 0.0 all-gather.2.cloned.1.call-start
  7.2 0.7 all-gather.2.cloned.1.call-update
  7.9 0.8 fusion.165
  8.7 1.3 %fusion.164 = (f32[2,6,8,8,2]{4,3,2,1,0:T(8,128)S(1)}, f32[2,6,8,8,2]{4,3,2,1,0:T(8,128)S(1)}) fusion(f32[2,6,8,8,128]{4,3,2,1,0:T(8,128)} %bitcast.388), kind=kLoop, calls=%fused_computation.388 | loop fusion | bytes 24576 | tf_op jit(solution)/shard_map/slice | solution.py:128
  10.1 0.1 copy.18
  10.2 0.2 reshape.590
  10.4 0.2 reshape.591
  10.6 0.1 copy.28
  10.7 0.1 copy.27
  10.8 0.7 pad_maximum_fusion.18
  11.6 5.6 %collective-permute-start = (f32[204,128]{0,1:T(8,128)}, f32[204,128]{0,1:T(8,128)S(1)}, u32[]{:S(2)}, u32[]{:S(2)}) collective-permute-start(f32[204,128]{0,1:T(8,128)} %get-tuple-element.79), channel_id=1, source_target_pairs={{0,1},{1,2},{2,3},{3,4},{4,5},{5,6},{6,7},{7,8},{8,9},{9,10},{10,1... | collective-permute-start | bytes 313352 | tf_op jit(solution)/shard_map/ppermute | solution.py:104
  17.2 10.9 %collective-permute-start.1 = (f32[204,128]{0,1:T(8,128)S(1)}, f32[204,128]{0,1:T(8,128)S(1)}, u32[]{:S(2)}, u32[]{:S(2)}) collective-permute-start(f32[204,128]{0,1:T(8,128)S(1)} %get-tuple-element.80), channel_id=1, source_target_pairs={{0,31},{1,0},{2,1},{3,2},{4,3},{5,4},{6,5},{7,6},{8,7},{9,8},{10,9... | collective-permute-start | bytes 313352 | tf_op jit(solution)/shard_map/ppermute | solution.py:104
  28.1 1.4 %fusion.176 = (s32[1,1,1]{1,2,0:T(1,128)}, s32[1,1,1]{1,2,0:T(1,128)}) fusion(s32[1,2,1]{1,2,0:T(1,128)} %param.6), kind=kLoop, calls=%fused_computation.400 | loop fusion | bytes 16 | tf_op jit(solution)/shard_map/slice | solution.py:134
  31.1 1.4 %fusion.177 = (s32[1,1,1]{1,2,0:T(1,128)}, s32[1,1,1]{1,2,0:T(1,128)}) fusion(s32[1,2,1]{1,2,0:T(1,128)} %param.7), kind=kLoop, calls=%fused_computation.401 | loop fusion | bytes 16 | tf_op jit(solution)/shard_map/slice | solution.py:139
  35.1 1.1 %fusion.108 = f32[2,8,8,128]{3,2,1,0:T(8,128)S(1)} fusion(f32[2,6,8,8,128]{4,3,2,1,0:T(8,128)} %bitcast.389), kind=kLoop, calls=%fused_computation.286 | loop fusion | flops 344064 | bytes 393216 | tf_op jit(solution)/shard_map/mul | solution.py:161
  36.2 1.1 %slice_bitcast_fusion.3 = (f32[6,8,8,128]{3,2,1,0:T(8,128)S(1)}, f32[6,8,8,128]{3,2,1,0:T(8,128)S(1)}) fusion(f32[1,2,6,8,8,128]{5,4,3,2,1,0:T(8,128)} %param.5), kind=kLoop, calls=%fused_computation.115 | loop fusion | bytes 786432 | tf_op jit(solution)/shard_map/squeeze | solution.py:153
  37.3 0.1 rev.13
  37.4 0.1 rev.12
  37.6 0.1 rev.15
  37.7 0.1 rev.14
  37.8 0.1 broadcast_multiply_fusion.6
  37.9 0.1 pad_maximum_fusion.5
  38.1 0.1 fusion.106
  38.2 0.1 fusion.87
  40.1 0.4 fusion.24
  40.5 0.4 fusion.10
  40.9 0.1 fusion.147
  40.9 0.1 fusion.168
  41.0 0.1 copy.19
  41.1 0.1 copy.23
  41.2 0.1 fusion.169
  41.3 0.1 copy.22
  41.4 0.1 copy.24
  41.5 0.1 fusion.112
  41.7 0.1 fusion.110
  41.8 3.6 %collective-permute-start.4 = (f32[192,128]{1,0:T(8,128)S(1)}, f32[192,128]{1,0:T(8,128)S(1)}, u32[]{:S(2)}, u32[]{:S(2)}) collective-permute-start(f32[192,128]{1,0:T(8,128)S(1)} %bitcast.408), channel_id=1, source_target_pairs={{0,28},{1,29},{2,30},{3,31},{4,0},{5,1},{6,2},{7,3},{8,4},{9,5},{1... | collective-permute-start | bytes 294920 | tf_op jit(solution)/shard_map/ppermute | solution.py:104
  45.4 2.6 %collective-permute-start.3 = (f32[192,128]{1,0:T(8,128)S(1)}, f32[192,128]{1,0:T(8,128)S(1)}, u32[]{:S(2)}, u32[]{:S(2)}) collective-permute-start(f32[192,128]{1,0:T(8,128)S(1)} %bitcast.409), channel_id=1, source_target_pairs={{0,30},{1,31},{2,0},{3,1},{4,2},{5,3},{6,4},{7,5},{8,6},{9,7},{10,... | collective-permute-start | bytes 294920 | tf_op jit(solution)/shard_map/ppermute | solution.py:104
  48.0 2.7 %collective-permute-start.2 = (f32[192,128]{1,0:T(8,128)S(1)}, f32[192,128]{1,0:T(8,128)S(1)}, u32[]{:S(2)}, u32[]{:S(2)}) collective-permute-start(f32[192,128]{1,0:T(8,128)S(1)} %bitcast.410), channel_id=1, source_target_pairs={{0,2},{1,3},{2,4},{3,5},{4,6},{5,7},{6,8},{7,9},{8,10},{9,11},{10,... | collective-permute-start | bytes 294920 | tf_op jit(solution)/shard_map/ppermute | solution.py:104
  50.7 0.1 slice.897
  50.8 0.1 reshape.588
  50.9 0.1 slice.898
  51.0 0.1 reshape.589
  51.1 1.1 %copy.26 = f32[2,6,8,8,2]{4,3,2,1,0:T(8,128)S(1)} copy(f32[2,6,8,8,2]{1,0,4,3,2:T(2,128)S(1)} %reshape.589) | data formatting | bytes 12288 | tf_op jit(solution)/shard_map/reshape | solution.py:107
  52.3 1.1 %copy.25 = f32[2,6,8,8,2]{4,3,2,1,0:T(8,128)S(1)} copy(f32[2,6,8,8,2]{1,0,4,3,2:T(2,128)S(1)} %reshape.588) | data formatting | bytes 12288 | tf_op jit(solution)/shard_map/reshape | solution.py:107
  53.4 0.4 pad_maximum_fusion
  53.8 0.1 fusion.93
  53.9 0.1 fusion.66
  54.0 0.1 add_divide_fusion.2
  54.2 0.1 add_divide_fusion
  54.3 0.1 subtract_maximum_fusion
  54.4 0.1 subtract_maximum_fusion.2
  54.7 0.1 slice_bitcast_fusion.1
  54.8 0.1 fusion.61
  55.1 7.0 %collective-permute-start.7 = (f32[192,128]{1,0:T(8,128)S(1)}, f32[192,128]{1,0:T(8,128)S(1)}, u32[]{:S(2)}, u32[]{:S(2)}) collective-permute-start(f32[192,128]{1,0:T(8,128)S(1)} %bitcast.411), channel_id=1, source_target_pairs={{0,16},{1,17},{2,18},{3,19},{4,20},{5,21},{6,22},{7,23},{8,24},{9,... | collective-permute-start | bytes 294920 | tf_op jit(solution)/shard_map/ppermute | solution.py:104
  62.1 1.1 %fusion.3 = (f32[6,8,8,129]{3,2,1,0:T(8,128)S(1)}, f32[6,8,8,129]{3,2,1,0:T(8,128)S(1)}) fusion(f32[6,8,8,132]{3,2,1,0:T(8,128)S(1)} %get-tuple-element.60, f32[6,8,8,132]{3,2,1,0:T(8,128)S(1)} %constant_dynamic-update-slice_fusion.30, f32[8,8,129]{2,1,0:T(8,128)S(1)} %get-tuple-element.44, f32[8,8,129]{2,1,0:T(8,128)S(1)} %get-tuple-element.45, ...), kind=kLoop, calls=%fused_computation.6 | loop fusion | flops 1287936 | bytes 2972160 | tf_op jit(solution)/shard_map/sub | solution.py:68
  63.2 2.4 %collective-permute-start.6 = (f32[192,128]{1,0:T(8,128)S(1)}, f32[192,128]{1,0:T(8,128)S(1)}, u32[]{:S(2)}, u32[]{:S(2)}) collective-permute-start(f32[192,128]{1,0:T(8,128)S(1)} %bitcast.412), channel_id=1, source_target_pairs={{0,24},{1,25},{2,26},{3,27},{4,28},{5,29},{6,30},{7,31},{8,0},{9,1... | collective-permute-start | bytes 294920 | tf_op jit(solution)/shard_map/ppermute | solution.py:104
  65.6 6.8 %collective-permute-start.5 = (f32[192,128]{1,0:T(8,128)S(1)}, f32[192,128]{1,0:T(8,128)S(1)}, u32[]{:S(2)}, u32[]{:S(2)}) collective-permute-start(f32[192,128]{1,0:T(8,128)S(1)} %bitcast.413), channel_id=1, source_target_pairs={{0,8},{1,9},{2,10},{3,11},{4,12},{5,13},{6,14},{7,15},{8,16},{9,17... | collective-permute-start | bytes 294920 | tf_op jit(solution)/shard_map/ppermute | solution.py:104
  72.4 11.5 %collective-permute-done.6 = f32[192,128]{1,0:T(8,128)S(1)} collective-permute-done((f32[192,128]{1,0:T(8,128)S(1)}, f32[192,128]{1,0:T(8,128)S(1)}, u32[]{:S(2)}, u32[]{:S(2)}) %collective-permute-start.6) | collective-permute-done | bytes 98336 | tf_op jit(solution)/shard_map/ppermute | solution.py:104
  84.5 0.1 fusion.42
  84.6 0.1 fusion.36
  84.7 0.1 fusion.51
  84.9 0.1 fusion.48
  85.0 3.6 %multiply_reduce_fusion = f32[2,6,8,8,128]{4,3,2,1,0:T(8,128)S(1)} fusion(f32[16,2,6,8,8,128]{5,4,3,2,1,0:T(8,128)} %all-gather.2.cloned.1.call-done, f32[16]{0:T(128)S(1)} %fusion.147), kind=kLoop, calls=%fused_computation | loop fusion | flops 3047424 | bytes 6684736 | tf_op jit(solution)/shard_map/reduce_sum | solution.py:152
  88.7 1.0 %multiply_subtract_fusion = (f32[1,2,6,8,8,128]{5,4,3,2,1,0:T(8,128)}, f32[1,2,6,8,8,128]{5,4,3,2,1,0:T(8,128)}) fusion(f32[1,2,6,8,8,128]{5,4,3,2,1,0:T(8,128)S(1)} %copy-done, f32[2,8,8,128]{3,2,1,0:T(8,128)S(1)} %fusion.108, f32[2,6,8,8,128]{4,3,2,1,0:T(8,128)S(1)} %multiply_reduce_fusion, f32[1,1,6,8,8,128]{5,4,3,2,1,0:T(8,128)S(1)} %fusion.48, ...), kind=kLoop, calls=%fused_computation.51 | loop fusion | flops 393216 | bytes 2031616 | tf_op jit(solution)/shard_map/sub | solution.py:161
  (86 shorter events, 1.3 us)
Async XLA Ops:
  7.2 30.6 %copy-start.1 = (f32[6]{0:T(128)S(1)}, f32[6]{0:T(128)}, u32[]{:S(2)}) copy-start(f32[6]{0:T(128)} %constant.251.clone) | copy-start | bytes 76
  7.2 77.9 %all-gather.2.cloned.1.call-start = ((), (), s32[]{:S(2)}) async-start(), calls=%async_computation | async-start | bytes 6684672 | tf_op jit(solution)/shard_map/all_gather | solution.py:149
  11.6 29.3 %collective-permute-start = (f32[204,128]{0,1:T(8,128)}, f32[204,128]{0,1:T(8,128)S(1)}, u32[]{:S(2)}, u32[]{:S(2)}) collective-permute-start(f32[204,128]{0,1:T(8,128)} %get-tuple-element.79), channel_id=1, source_target_pairs={{0,1},{1,2},{2,3},{3,4},{4,5},{5,6},{6,7},{7,8},{8,9},{9,10},{10,1... | collective-permute-start | bytes 313352 | tf_op jit(solution)/shard_map/ppermute | solution.py:104
  17.2 24.0 %collective-permute-start.1 = (f32[204,128]{0,1:T(8,128)S(1)}, f32[204,128]{0,1:T(8,128)S(1)}, u32[]{:S(2)}, u32[]{:S(2)}) collective-permute-start(f32[204,128]{0,1:T(8,128)S(1)} %get-tuple-element.80), channel_id=1, source_target_pairs={{0,31},{1,0},{2,1},{3,2},{4,3},{5,4},{6,5},{7,6},{8,7},{9,8},{10,9... | collective-permute-start | bytes 313352 | tf_op jit(solution)/shard_map/ppermute | solution.py:104
  38.2 15.2 %copy-start = (f32[1,2,6,8,8,128]{5,4,3,2,1,0:T(8,128)S(1)}, f32[1,2,6,8,8,128]{5,4,3,2,1,0:T(8,128)}, u32[]{:S(2)}) copy-start(f32[1,2,6,8,8,128]{5,4,3,2,1,0:T(8,128)} %param.5) | copy-start | bytes 1179652
  41.8 13.1 %collective-permute-start.4 = (f32[192,128]{1,0:T(8,128)S(1)}, f32[192,128]{1,0:T(8,128)S(1)}, u32[]{:S(2)}, u32[]{:S(2)}) collective-permute-start(f32[192,128]{1,0:T(8,128)S(1)} %bitcast.408), channel_id=1, source_target_pairs={{0,28},{1,29},{2,30},{3,31},{4,0},{5,1},{6,2},{7,3},{8,4},{9,5},{1... | collective-permute-start | bytes 294920 | tf_op jit(solution)/shard_map/ppermute | solution.py:104
  45.4 9.5 %collective-permute-start.3 = (f32[192,128]{1,0:T(8,128)S(1)}, f32[192,128]{1,0:T(8,128)S(1)}, u32[]{:S(2)}, u32[]{:S(2)}) collective-permute-start(f32[192,128]{1,0:T(8,128)S(1)} %bitcast.409), channel_id=1, source_target_pairs={{0,30},{1,31},{2,0},{3,1},{4,2},{5,3},{6,4},{7,5},{8,6},{9,7},{10,... | collective-permute-start | bytes 294920 | tf_op jit(solution)/shard_map/ppermute | solution.py:104
  48.0 6.9 %collective-permute-start.2 = (f32[192,128]{1,0:T(8,128)S(1)}, f32[192,128]{1,0:T(8,128)S(1)}, u32[]{:S(2)}, u32[]{:S(2)}) collective-permute-start(f32[192,128]{1,0:T(8,128)S(1)} %bitcast.410), channel_id=1, source_target_pairs={{0,2},{1,3},{2,4},{3,5},{4,6},{5,7},{6,8},{7,9},{8,10},{9,11},{10,... | collective-permute-start | bytes 294920 | tf_op jit(solution)/shard_map/ppermute | solution.py:104
  55.1 17.3 %collective-permute-start.7 = (f32[192,128]{1,0:T(8,128)S(1)}, f32[192,128]{1,0:T(8,128)S(1)}, u32[]{:S(2)}, u32[]{:S(2)}) collective-permute-start(f32[192,128]{1,0:T(8,128)S(1)} %bitcast.411), channel_id=1, source_target_pairs={{0,16},{1,17},{2,18},{3,19},{4,20},{5,21},{6,22},{7,23},{8,24},{9,... | collective-permute-start | bytes 294920 | tf_op jit(solution)/shard_map/ppermute | solution.py:104
  63.2 20.7 %collective-permute-start.6 = (f32[192,128]{1,0:T(8,128)S(1)}, f32[192,128]{1,0:T(8,128)S(1)}, u32[]{:S(2)}, u32[]{:S(2)}) collective-permute-start(f32[192,128]{1,0:T(8,128)S(1)} %bitcast.412), channel_id=1, source_target_pairs={{0,24},{1,25},{2,26},{3,27},{4,28},{5,29},{6,30},{7,31},{8,0},{9,1... | collective-permute-start | bytes 294920 | tf_op jit(solution)/shard_map/ppermute | solution.py:104
  65.6 18.3 %collective-permute-start.5 = (f32[192,128]{1,0:T(8,128)S(1)}, f32[192,128]{1,0:T(8,128)S(1)}, u32[]{:S(2)}, u32[]{:S(2)}) collective-permute-start(f32[192,128]{1,0:T(8,128)S(1)} %bitcast.413), channel_id=1, source_target_pairs={{0,8},{1,9},{2,10},{3,11},{4,12},{5,13},{6,14},{7,15},{8,16},{9,17... | collective-permute-start | bytes 294920 | tf_op jit(solution)/shard_map/ppermute | solution.py:104
Sparse Core Ops, SparseCore 0:
  10.1 55.6 all-gather.1

commit v4 on v3

--- a/solution.py
+++ b/solution.py
@@ -113,6 +113,13 @@
     return lax.dynamic_index_in_dim(jnp.stack(candidates), index, 0, keepdims=False)
 
 
+def select_chain(candidates, index):
+    chosen = candidates[0]
+    for k in range(1, len(candidates)):
+        chosen = jnp.where(index == k, candidates[k], chosen)
+    return chosen
+
+
 def signed_digit(value, radix):
     return jnp.mod(value + 1, radix) - 1
 
@@ -136,16 +143,15 @@
         rest = jnp.mod((rotation - low) // 2, total_blocks // 2)
         mid_digit.append(signed_digit(rest, 4))
         top_digit.append(signed_digit(jnp.mod((rest - mid_digit[t]) // 4, 4), 4))
-        offset = donor_offset[0, t, 0] + 0 * rotation
         first = pick([c[t] for c in near], low + 1)
         second = pick([c[t] for c in near], low + 2)
         joined = jnp.concatenate([first, second], axis=-1)
-        windows.append(lax.dynamic_slice_in_dim(joined, offset, width, axis=-1))
+        windows.append(lax.dynamic_slice_in_dim(joined, donor_offset[0, t, 0], width, axis=-1))
     windows = jnp.stack(windows)
     mid = [shifted([windows], -2)[0], windows] + [shifted([windows], s)[0] for s in (2, 4)]
     windows = jnp.stack([pick([c[t] for c in mid], mid_digit[t] + 1) for t in range(2)])
     top = [shifted([windows], -8)[0], windows] + [shifted([windows], s)[0] for s in (8, 16)]
-    rotor_high, stator_low = [pick([c[t] for c in top], top_digit[t] + 1) for t in range(2)]
+    rotor_high, stator_low = [select_chain([c[t] for c in top], top_digit[t] + 1) for t in range(2)]
     piece = lax.all_gather(state, "inst", axis=0, tiled=True)
     sources = jnp.arange(piece.shape[0], dtype=jnp.int32)
     weights = spectral_weights(own_instance, sources, number)

time: 97.1 us -> 100 us (1.030)
  the two profiles are of different devices: /device:TPU:1 before, /device:TPU:38 now
where the time goes in v4:
time: 100 us; the launch traced here: 99.5 us
  starting transfers between devices  42.3 us (42%)
  between operations  20.6 us (21%)
  waiting for transfers between devices  14.6 us (15%)
  other arithmetic  11.4 us (11%)
  local copies, waits for them, and re-layouts  10.6 us (11%)
    ppermute x8, starting transfers between devices, shifted(): lax.ppermute(jnp.concatenate(rows, axis=0) if len(rows) > 1 else rows[0],...  42.3 us
    ppermute x8, waiting for transfers between devices, shifted(): lax.ppermute(jnp.concatenate(rows, axis=0) if len(rows) > 1 else rows[0],...  13.9 us
    reduce_sum x1, other arithmetic, per_device(): jnp.sum(weights.reshape((-1,) + (1,) * (piece.ndim - 1)) * piece, axis=0)  3.62 us
    reshape x4, local copies, waits for them, and re-layouts, shifted(): pieces.append(moved[begin:begin + size].reshape(p.shape))  2.51 us
    sub x5, other arithmetic, flux_divergence(): 0.5 * (take_range(fluxes, 1, length + 1, along) + take_range(fluxes, 2, l...  2.02 us
  transfers between devices with their start and end apart: 9, of which 1 were waited for; matrix products, arithmetic and copies ran while one was open for 18% of the time, Pallas kernels for 0%

profile of v4, /device:TPU:38, one launch (start us, length us, event | category | flops | bytes accessed | tf_op | source)
XLA Modules:
  0.0 99.5 jit_solution(4384760353370337318)
XLA Ops:
  7.2 0.0 all-gather.2.cloned.1.call-start
  7.2 0.7 all-gather.2.cloned.1.call-update
  7.9 0.8 fusion.161
  8.7 1.3 %fusion.160 = (f32[2,6,8,8,2]{4,3,2,1,0:T(8,128)S(1)}, f32[2,6,8,8,2]{4,3,2,1,0:T(8,128)S(1)}) fusion(f32[2,6,8,8,128]{4,3,2,1,0:T(8,128)} %bitcast.396), kind=kLoop, calls=%fused_computation.378 | loop fusion | bytes 24576 | tf_op jit(solution)/shard_map/slice | solution.py:135
  10.1 0.1 copy.18
  10.2 0.2 reshape.596
  10.4 0.2 reshape.597
  10.6 0.1 copy.28
  10.7 0.1 copy.27
  10.8 0.7 pad_maximum_fusion.18
  11.6 5.1 %collective-permute-start = (f32[204,128]{0,1:T(8,128)}, f32[204,128]{0,1:T(8,128)S(1)}, u32[]{:S(2)}, u32[]{:S(2)}) collective-permute-start(f32[204,128]{0,1:T(8,128)} %get-tuple-element.79), channel_id=1, source_target_pairs={{0,1},{1,2},{2,3},{3,4},{4,5},{5,6},{6,7},{7,8},{8,9},{9,10},{10,1... | collective-permute-start | bytes 313352 | tf_op jit(solution)/shard_map/ppermute | solution.py:104
  16.7 3.1 %collective-permute-start.1 = (f32[204,128]{0,1:T(8,128)S(1)}, f32[204,128]{0,1:T(8,128)S(1)}, u32[]{:S(2)}, u32[]{:S(2)}) collective-permute-start(f32[204,128]{0,1:T(8,128)S(1)} %get-tuple-element.80), channel_id=1, source_target_pairs={{0,31},{1,0},{2,1},{3,2},{4,3},{5,4},{6,5},{7,6},{8,7},{9,8},{10,9... | collective-permute-start | bytes 313352 | tf_op jit(solution)/shard_map/ppermute | solution.py:104
  19.8 1.4 %fusion.172 = (s32[1,1,1]{1,2,0:T(1,128)}, s32[1,1,1]{1,2,0:T(1,128)}) fusion(s32[1,2,1]{1,2,0:T(1,128)} %param.6), kind=kLoop, calls=%fused_computation.390 | loop fusion | bytes 16 | tf_op jit(solution)/shard_map/slice | solution.py:141
  22.8 1.4 %fusion.173 = (s32[1,1,1]{1,2,0:T(1,128)}, s32[1,1,1]{1,2,0:T(1,128)}) fusion(s32[1,2,1]{1,2,0:T(1,128)} %param.7), kind=kLoop, calls=%fused_computation.391 | loop fusion | bytes 16 | tf_op jit(solution)/shard_map/slice | solution.py:149
  26.9 1.1 %fusion.108 = f32[2,8,8,128]{3,2,1,0:T(8,128)S(1)} fusion(f32[2,6,8,8,128]{4,3,2,1,0:T(8,128)} %bitcast.397), kind=kLoop, calls=%fused_computation.278 | loop fusion | flops 344064 | bytes 393216 | tf_op jit(solution)/shard_map/mul | solution.py:167
  27.9 1.1 %slice_bitcast_fusion.3 = (f32[6,8,8,128]{3,2,1,0:T(8,128)S(1)}, f32[6,8,8,128]{3,2,1,0:T(8,128)S(1)}) fusion(f32[1,2,6,8,8,128]{5,4,3,2,1,0:T(8,128)} %param.5), kind=kLoop, calls=%fused_computation.107 | loop fusion | bytes 786432 | tf_op jit(solution)/shard_map/squeeze | solution.py:159
  29.1 0.1 rev.13
  29.2 0.1 rev.12
  29.3 0.1 rev.15
  29.4 0.1 rev.14
  29.6 0.1 broadcast_multiply_fusion.6
  29.7 0.1 pad_maximum_fusion.5
  29.9 0.1 fusion.106
  29.9 0.1 fusion.87
  31.8 0.4 fusion.24
  32.2 0.4 fusion.10
  32.6 0.1 fusion.143
  32.7 0.1 fusion.164
  32.7 0.1 copy.19
  32.8 0.1 copy.23
  32.9 0.1 fusion.165
  33.0 0.1 copy.22
  33.1 0.1 copy.24
  33.3 0.1 fusion.112
  33.4 0.1 fusion.110
  33.5 11.0 %collective-permute-start.4 = (f32[192,128]{1,0:T(8,128)S(1)}, f32[192,128]{1,0:T(8,128)S(1)}, u32[]{:S(2)}, u32[]{:S(2)}) collective-permute-start(f32[192,128]{1,0:T(8,128)S(1)} %bitcast.416), channel_id=1, source_target_pairs={{0,28},{1,29},{2,30},{3,31},{4,0},{5,1},{6,2},{7,3},{8,4},{9,5},{1... | collective-permute-start | bytes 294920 | tf_op jit(solution)/shard_map/ppermute | solution.py:104
  44.5 2.9 %collective-permute-start.3 = (f32[192,128]{1,0:T(8,128)S(1)}, f32[192,128]{1,0:T(8,128)S(1)}, u32[]{:S(2)}, u32[]{:S(2)}) collective-permute-start(f32[192,128]{1,0:T(8,128)S(1)} %bitcast.417), channel_id=1, source_target_pairs={{0,30},{1,31},{2,0},{3,1},{4,2},{5,3},{6,4},{7,5},{8,6},{9,7},{10,... | collective-permute-start | bytes 294920 | tf_op jit(solution)/shard_map/ppermute | solution.py:104
  47.4 2.9 %collective-permute-start.2 = (f32[192,128]{1,0:T(8,128)S(1)}, f32[192,128]{1,0:T(8,128)S(1)}, u32[]{:S(2)}, u32[]{:S(2)}) collective-permute-start(f32[192,128]{1,0:T(8,128)S(1)} %bitcast.418), channel_id=1, source_target_pairs={{0,2},{1,3},{2,4},{3,5},{4,6},{5,7},{6,8},{7,9},{8,10},{9,11},{10,... | collective-permute-start | bytes 294920 | tf_op jit(solution)/shard_map/ppermute | solution.py:104
  50.3 0.1 slice.879
  50.4 0.1 reshape.594
  50.5 0.1 slice.880
  50.6 0.1 reshape.595
  50.8 1.1 %copy.26 = f32[2,6,8,8,2]{4,3,2,1,0:T(8,128)S(1)} copy(f32[2,6,8,8,2]{1,0,4,3,2:T(2,128)S(1)} %reshape.595) | data formatting | bytes 12288 | tf_op jit(solution)/shard_map/reshape | solution.py:107
  51.9 1.1 %copy.25 = f32[2,6,8,8,2]{4,3,2,1,0:T(8,128)S(1)} copy(f32[2,6,8,8,2]{1,0,4,3,2:T(2,128)S(1)} %reshape.594) | data formatting | bytes 12288 | tf_op jit(solution)/shard_map/reshape | solution.py:107
  53.0 0.4 pad_maximum_fusion
  53.4 0.1 fusion.93
  53.5 0.1 fusion.66
  53.6 0.1 add_divide_fusion.2
  53.8 0.1 add_divide_fusion
  53.9 0.1 subtract_maximum_fusion
  54.0 0.1 subtract_maximum_fusion.2
  54.3 0.1 slice_bitcast_fusion.1
  54.4 0.1 fusion.61
  54.7 1.9 %collective-permute-start.7 = (f32[192,128]{1,0:T(8,128)S(1)}, f32[192,128]{1,0:T(8,128)S(1)}, u32[]{:S(2)}, u32[]{:S(2)}) collective-permute-start(f32[192,128]{1,0:T(8,128)S(1)} %bitcast.419), channel_id=1, source_target_pairs={{0,8},{1,9},{2,10},{3,11},{4,12},{5,13},{6,14},{7,15},{8,16},{9,17... | collective-permute-start | bytes 294920 | tf_op jit(solution)/shard_map/ppermute | solution.py:104
  56.6 1.1 %fusion.3 = (f32[6,8,8,129]{3,2,1,0:T(8,128)S(1)}, f32[6,8,8,129]{3,2,1,0:T(8,128)S(1)}) fusion(f32[6,8,8,132]{3,2,1,0:T(8,128)S(1)} %get-tuple-element.60, f32[6,8,8,132]{3,2,1,0:T(8,128)S(1)} %constant_dynamic-update-slice_fusion.30, f32[8,8,129]{2,1,0:T(8,128)S(1)} %get-tuple-element.44, f32[8,8,129]{2,1,0:T(8,128)S(1)} %get-tuple-element.45, ...), kind=kLoop, calls=%fused_computation.6 | loop fusion | flops 1287936 | bytes 2972160 | tf_op jit(solution)/shard_map/sub | solution.py:68
  57.7 7.8 %collective-permute-start.6 = (f32[192,128]{1,0:T(8,128)S(1)}, f32[192,128]{1,0:T(8,128)S(1)}, u32[]{:S(2)}, u32[]{:S(2)}) collective-permute-start(f32[192,128]{1,0:T(8,128)S(1)} %bitcast.420), channel_id=1, source_target_pairs={{0,24},{1,25},{2,26},{3,27},{4,28},{5,29},{6,30},{7,31},{8,0},{9,1... | collective-permute-start | bytes 294920 | tf_op jit(solution)/shard_map/ppermute | solution.py:104
  65.5 7.5 %collective-permute-start.5 = (f32[192,128]{1,0:T(8,128)S(1)}, f32[192,128]{1,0:T(8,128)S(1)}, u32[]{:S(2)}, u32[]{:S(2)}) collective-permute-start(f32[192,128]{1,0:T(8,128)S(1)} %bitcast.421), channel_id=1, source_target_pairs={{0,16},{1,17},{2,18},{3,19},{4,20},{5,21},{6,22},{7,23},{8,24},{9,... | collective-permute-start | bytes 294920 | tf_op jit(solution)/shard_map/ppermute | solution.py:104
  73.1 13.9 %collective-permute-done.5 = f32[192,128]{1,0:T(8,128)S(1)} collective-permute-done((f32[192,128]{1,0:T(8,128)S(1)}, f32[192,128]{1,0:T(8,128)S(1)}, u32[]{:S(2)}, u32[]{:S(2)}) %collective-permute-start.5) | collective-permute-done | bytes 98336 | tf_op jit(solution)/shard_map/ppermute | solution.py:104
  87.6 0.1 fusion.42
  87.7 0.1 fusion.36
  87.8 0.1 fusion.51
  87.9 0.1 fusion.48
  88.1 3.6 %multiply_reduce_fusion = f32[2,6,8,8,128]{4,3,2,1,0:T(8,128)S(1)} fusion(f32[16,2,6,8,8,128]{5,4,3,2,1,0:T(8,128)} %all-gather.2.cloned.1.call-done, f32[16]{0:T(128)S(1)} %fusion.143), kind=kLoop, calls=%fused_computation | loop fusion | flops 3047424 | bytes 6684736 | tf_op jit(solution)/shard_map/reduce_sum | solution.py:158
  91.7 1.0 multiply_subtract_fusion
  (86 shorter events, 1.3 us)
Async XLA Ops:
  7.2 22.4 %copy-start.1 = (f32[6]{0:T(128)S(1)}, f32[6]{0:T(128)}, u32[]{:S(2)}) copy-start(f32[6]{0:T(128)} %constant.244.clone) | copy-start | bytes 76
  7.2 80.9 %all-gather.2.cloned.1.call-start = ((), (), s32[]{:S(2)}) async-start(), calls=%async_computation | async-start | bytes 6684672 | tf_op jit(solution)/shard_map/all_gather | solution.py:155
  11.6 21.1 %collective-permute-start = (f32[204,128]{0,1:T(8,128)}, f32[204,128]{0,1:T(8,128)S(1)}, u32[]{:S(2)}, u32[]{:S(2)}) collective-permute-start(f32[204,128]{0,1:T(8,128)} %get-tuple-element.79), channel_id=1, source_target_pairs={{0,1},{1,2},{2,3},{3,4},{4,5},{5,6},{6,7},{7,8},{8,9},{9,10},{10,1... | collective-permute-start | bytes 313352 | tf_op jit(solution)/shard_map/ppermute | solution.py:104
  16.7 16.3 %collective-permute-start.1 = (f32[204,128]{0,1:T(8,128)S(1)}, f32[204,128]{0,1:T(8,128)S(1)}, u32[]{:S(2)}, u32[]{:S(2)}) collective-permute-start(f32[204,128]{0,1:T(8,128)S(1)} %get-tuple-element.80), channel_id=1, source_target_pairs={{0,31},{1,0},{2,1},{3,2},{4,3},{5,4},{6,5},{7,6},{8,7},{9,8},{10,9... | collective-permute-start | bytes 313352 | tf_op jit(solution)/shard_map/ppermute | solution.py:104
  30.0 23.0 %copy-start = (f32[1,2,6,8,8,128]{5,4,3,2,1,0:T(8,128)S(1)}, f32[1,2,6,8,8,128]{5,4,3,2,1,0:T(8,128)}, u32[]{:S(2)}) copy-start(f32[1,2,6,8,8,128]{5,4,3,2,1,0:T(8,128)} %param.5) | copy-start | bytes 1179652
  33.5 21.0 %collective-permute-start.4 = (f32[192,128]{1,0:T(8,128)S(1)}, f32[192,128]{1,0:T(8,128)S(1)}, u32[]{:S(2)}, u32[]{:S(2)}) collective-permute-start(f32[192,128]{1,0:T(8,128)S(1)} %bitcast.416), channel_id=1, source_target_pairs={{0,28},{1,29},{2,30},{3,31},{4,0},{5,1},{6,2},{7,3},{8,4},{9,5},{1... | collective-permute-start | bytes 294920 | tf_op jit(solution)/shard_map/ppermute | solution.py:104
  44.5 10.1 %collective-permute-start.3 = (f32[192,128]{1,0:T(8,128)S(1)}, f32[192,128]{1,0:T(8,128)S(1)}, u32[]{:S(2)}, u32[]{:S(2)}) collective-permute-start(f32[192,128]{1,0:T(8,128)S(1)} %bitcast.417), channel_id=1, source_target_pairs={{0,30},{1,31},{2,0},{3,1},{4,2},{5,3},{6,4},{7,5},{8,6},{9,7},{10,... | collective-permute-start | bytes 294920 | tf_op jit(solution)/shard_map/ppermute | solution.py:104
  47.4 7.2 %collective-permute-start.2 = (f32[192,128]{1,0:T(8,128)S(1)}, f32[192,128]{1,0:T(8,128)S(1)}, u32[]{:S(2)}, u32[]{:S(2)}) collective-permute-start(f32[192,128]{1,0:T(8,128)S(1)} %bitcast.418), channel_id=1, source_target_pairs={{0,2},{1,3},{2,4},{3,5},{4,6},{5,7},{6,8},{7,9},{8,10},{9,11},{10,... | collective-permute-start | bytes 294920 | tf_op jit(solution)/shard_map/ppermute | solution.py:104
  54.7 18.4 %collective-permute-start.7 = (f32[192,128]{1,0:T(8,128)S(1)}, f32[192,128]{1,0:T(8,128)S(1)}, u32[]{:S(2)}, u32[]{:S(2)}) collective-permute-start(f32[192,128]{1,0:T(8,128)S(1)} %bitcast.419), channel_id=1, source_target_pairs={{0,8},{1,9},{2,10},{3,11},{4,12},{5,13},{6,14},{7,15},{8,16},{9,17... | collective-permute-start | bytes 294920 | tf_op jit(solution)/shard_map/ppermute | solution.py:104
  57.7 15.4 %collective-permute-start.6 = (f32[192,128]{1,0:T(8,128)S(1)}, f32[192,128]{1,0:T(8,128)S(1)}, u32[]{:S(2)}, u32[]{:S(2)}) collective-permute-start(f32[192,128]{1,0:T(8,128)S(1)} %bitcast.420), channel_id=1, source_target_pairs={{0,24},{1,25},{2,26},{3,27},{4,28},{5,29},{6,30},{7,31},{8,0},{9,1... | collective-permute-start | bytes 294920 | tf_op jit(solution)/shard_map/ppermute | solution.py:104
  65.5 21.4 %collective-permute-start.5 = (f32[192,128]{1,0:T(8,128)S(1)}, f32[192,128]{1,0:T(8,128)S(1)}, u32[]{:S(2)}, u32[]{:S(2)}) collective-permute-start(f32[192,128]{1,0:T(8,128)S(1)} %bitcast.421), channel_id=1, source_target_pairs={{0,16},{1,17},{2,18},{3,19},{4,20},{5,21},{6,22},{7,23},{8,24},{9,... | collective-permute-start | bytes 294920 | tf_op jit(solution)/shard_map/ppermute | solution.py:104
Sparse Core Ops, SparseCore 0:
  10.1 53.8 all-gather.1
